TPU v7x, 32 devices: a whole 2x2x4 slice. The times are simulated.
32 devices in a mesh: grp: 2 (over x), spec: 16 (over z, y, core).
Axes of the slice: x: 2, y: 2, z: 4, core: 2. Of those that a mesh axis runs over, the one named last changes fastest.
Arguments:
- lower_coef: bfloat16 [64, 196, 1024], P(('grp', 'spec')), parts along dimension 0, may hold values from -6 to 6
- upper_coef: bfloat16 [64, 196, 1024], P(('grp', 'spec')), parts along dimension 0, may hold values from -6 to 6
- w_down: bfloat16 [4096, 1024], P('spec'), may hold values from -0.09375 to 0.09375
- w_up: bfloat16 [4096, 1024], P('spec'), may hold values from -0.1875 to 0.1875
- pw1_bias: bfloat16 [4096], P('spec'), may hold values from -0.059814453 to 0.059814453
- slopes: bfloat16 [8192, 2, 196], P(('grp', 'spec')), parts along dimension 0, may hold values from -0.099609375 to 1.09375
- intercepts: bfloat16 [8192, 2, 196], P(('grp', 'spec')), parts along dimension 0, may hold values from -0.019897461 to 0.019897461
- ln_scale: float32 [392], P('grp'), parts along dimension 0, may hold values from 0.3 to 3
- box_center: float32 [392, 1024], P('grp', 'spec'), parts along dimension 0, may hold values from -0.03 to 0.03
- box_radius: float32 [392, 1024], P('grp', 'spec'), parts along dimension 0, may hold values from 1e-06 to 0.0001
- dw_weight: float32 [49, 1024], P(None, 'spec'), may hold values from -0.875 to 0.875
- dw_bias: float32 [1024], P('spec'), may hold values from -0.06 to 0.06
- ln_gain: float32 [1024], P('spec'), may hold values from 0.5 to 1.5
- ln_bias: float32 [1024], P('spec'), may hold values from -0.06 to 0.06
- ls_gamma: float32 [1024], P('spec'), may hold values from 0.1 to 1
- pw2_bias: float32 [1024], P('spec'), may hold values from -0.06 to 0.06
Outputs:
- lower_input: bfloat16 [64, 196, 1024], P(('grp', 'spec')), parts along dimension 0
- upper_input: bfloat16 [64, 196, 1024], P(('grp', 'spec')), parts along dimension 0
- bounds: float32 [64, 2], P(('grp', 'spec')), parts along dimension 0
There are 2 independent parts, one for each index of `grp`. A program takes and returns all parts, laid end to end along the dimension named above; an argument that names none is the same for every part. Nothing has to cross between parts.
All inputs are finite; a program needn't handle non-finite values.
Results may differ from a plain program's by a relative error of at most 0.0039.
Values may be sent and summed in bfloat16 or wider, within the bound.
No kernel may reach another device: no remote copies, remote signals or barrier semaphores. Data moves between devices by JAX's collectives and lax.ppermute only.
A program may use at most 192 MiB of HBM per device.

v0:
```python
import jax
import jax.numpy as jnp
from jax import lax
from jax.sharding import PartitionSpec as P

MAP = 14
KERNEL = 7


def conv_back(centered, taps):
    half = KERNEL // 2
    padded = jnp.pad(centered, ((0, 0), (half, half), (half, half), (0, 0)))
    result = jnp.zeros(centered.shape, jnp.float32)
    for row_off in range(KERNEL):
        for col_off in range(KERNEL):
            window = padded[
                :,
                2 * half - row_off : 2 * half - row_off + MAP,
                2 * half - col_off : 2 * half - col_off + MAP,
                :,
            ]
            result = result + window * taps[row_off, col_off]
    return result


def local(
    lower_coef,
    upper_coef,
    w_down,
    w_up,
    pw1_bias,
    slopes,
    intercepts,
    ln_scale,
    box_center,
    box_radius,
    dw_weight,
    dw_bias,
    ln_gain,
    ln_bias,
    ls_gamma,
    pw2_bias,
):
    center, radius, kernel_taps, conv_bias, gain, norm_bias, gamma, out_bias = (
        lax.all_gather(box_center, "spec", axis=1, tiled=True),
        lax.all_gather(box_radius, "spec", axis=1, tiled=True),
        lax.all_gather(dw_weight, "spec", axis=1, tiled=True),
        lax.all_gather(dw_bias, "spec", axis=0, tiled=True),
        lax.all_gather(ln_gain, "spec", axis=0, tiled=True),
        lax.all_gather(ln_bias, "spec", axis=0, tiled=True),
        lax.all_gather(ls_gamma, "spec", axis=0, tiled=True),
        lax.all_gather(pw2_bias, "spec", axis=0, tiled=True),
    )
    nrows = lower_coef.shape[0]
    npix = lower_coef.shape[1]
    chans = lower_coef.shape[2]
    height = 2 * nrows * npix
    coef = jnp.stack([lower_coef, upper_coef]).astype(jnp.float32)
    scaled = coef * gamma
    bias = jnp.sum(scaled * out_bias, axis=(2, 3))
    flat = scaled.astype(jnp.bfloat16).reshape(height, chans)
    hidden = jnp.dot(
        flat,
        lax.all_gather(w_down, "spec", axis=0, tiled=True).T,
        preferred_element_type=jnp.float32,
    ).reshape(2, nrows, npix, -1)
    slope_f = (
        lax.all_gather(slopes, "spec", axis=0, tiled=True).astype(jnp.float32).transpose(1, 2, 0)
    )
    icpt_f = (
        lax.all_gather(intercepts, "spec", axis=0, tiled=True)
        .astype(jnp.float32)
        .transpose(1, 2, 0)
    )
    first = jnp.stack([slope_f[0], slope_f[1]])[:, None]
    second = jnp.stack([slope_f[1], slope_f[0]])[:, None]
    first_icpt = jnp.stack([icpt_f[0], icpt_f[1]])[:, None]
    second_icpt = jnp.stack([icpt_f[1], icpt_f[0]])[:, None]
    positive = jnp.maximum(hidden, 0.0)
    negative = jnp.minimum(hidden, 0.0)
    relaxed = positive * first + negative * second
    extra = jnp.sum(
        positive * first_icpt
        + negative * second_icpt
        + relaxed * lax.all_gather(pw1_bias, "spec", axis=0, tiled=True).astype(jnp.float32),
        axis=(2, 3),
    )
    relaxed16, extra = (relaxed.astype(jnp.bfloat16).reshape(height, -1), extra)
    normed, extra = (
        jnp.dot(
            relaxed16,
            lax.all_gather(w_up, "spec", axis=0, tiled=True),
            preferred_element_type=jnp.float32,
        ),
        extra,
    )
    bias = bias + extra
    normed = normed.reshape(2, nrows, npix, chans)
    bias = bias + jnp.sum(normed * norm_bias, axis=(2, 3))
    tilted = normed * gain
    centered = ln_scale[None, None, :, None] * (tilted - jnp.mean(tilted, axis=-1, keepdims=True))
    bias = bias + jnp.sum(centered * conv_bias, axis=(2, 3))
    taps = kernel_taps.reshape(KERNEL, KERNEL, chans)
    conv = conv_back(centered.reshape(2 * nrows, MAP, MAP, chans), taps).reshape(
        2, nrows, npix, chans
    )
    total = coef + conv
    linear = jnp.sum(total * center, axis=(2, 3))
    spread = jnp.sum(jnp.abs(total) * radius, axis=(2, 3))
    bounds = bias + linear + jnp.stack([-spread[0], spread[1]])
    return (total[0].astype(jnp.bfloat16), total[1].astype(jnp.bfloat16), bounds.T)


def solution(mesh):
    placed = (
        P(("grp", "spec"), None, None),
        P(("grp", "spec"), None, None),
        P("spec", None),
        P("spec", None),
        P("spec"),
        P(("grp", "spec"), None, None),
        P(("grp", "spec"), None, None),
        P("grp"),
        P("grp", "spec"),
        P("grp", "spec"),
        P(None, "spec"),
        P("spec"),
        P("spec"),
        P("spec"),
        P("spec"),
        P("spec"),
    )
    return jax.shard_map(
        local,
        mesh=mesh,
        in_specs=placed,
        out_specs=(
            P(("grp", "spec"), None, None),
            P(("grp", "spec"), None, None),
            P(("grp", "spec"), None),
        ),
        check_vma=False,
    )
```

profile of v0, /device:TPU:0, one launch (start us, length us, event | category | flops | bytes accessed | tf_op | source)
XLA Modules:
  0.0 399.0 jit_solution(6297640007697791698)
XLA Ops:
  7.2 0.0 all-gather.9.cloned.1.call-start
  7.2 0.7 all-gather.9.cloned.1.call-update
  7.9 0.0 all-gather.13.cloned.1.call-start
  7.9 0.7 all-gather.13.cloned.1.call-update
  8.6 0.0 all-gather.7.cloned.1.call-start
  8.7 0.7 all-gather.7.cloned.1.call-update
  9.4 0.0 all-gather.11.cloned.1.call-start
  9.4 0.5 all-gather.11.cloned.1.call-update
  10.0 0.7 reshape.130
  10.6 23.1 %all-gather.1 = bf16[16,1,256]{2,1,0:T(2,128)(2,1)S(1)} all-gather(bf16[1,1,256]{2,1,0:T(2,128)(2,1)S(1)} %reshape.130), channel_id=1, replica_groups=mesh['grp'=2,'spec'=16] {'spec'}, dimensions={0}, use_global_device_ids=true | all-gather | bytes 8704 | tf_op jit(solution)/shard_map/all_gather | solution.py:85
  33.7 21.0 %all-gather = f32[16,64,49]{1,2,0:T(8,128)S(1)} all-gather(f32[1,64,49]{1,2,0:T(8,128)} %bitcast.99), channel_id=1, replica_groups=mesh['grp'=2,'spec'=16] {'spec'}, dimensions={0}, use_global_device_ids=true | all-gather | bytes 213248 | tf_op jit(solution)/shard_map/all_gather | solution.py:47
  54.8 0.1 copy.41
  54.8 0.2 reshape.129
  55.0 0.7 reshape.110
  55.7 3.1 fusion.108
  58.8 0.0 copy-start.3
  58.8 4.0 %reshape.112 = f32[4,14,14,1024]{3,0,2,1:T(4,128)} reshape(f32[2,2,196,1024]{3,1,0,2:T(2,128)S(1)} %fusion.108) | data formatting | bytes 6422528 | tf_op jit(solution)/shard_map/convert_element_type | solution.py:58
  62.8 22.8 %all_gather.50 = f32[196,1024]{0,1:T(8,128)S(1)} all-gather(f32[196,64]{0,1:T(8,128)S(1)} %copy-done.3), channel_id=1, replica_groups=mesh['grp'=2,'spec'=16] {'spec'}, dimensions={1}, use_global_device_ids=true | all-gather | bytes 852992 | tf_op jit(solution)/shard_map/all_gather | solution.py:45
  85.7 0.3 copy.44
  86.0 0.0 copy-start.11
  86.0 0.0 copy-start.6
  86.0 0.0 copy-start.7
  86.0 0.0 copy-start.8
  86.1 0.0 copy-start.9
  86.1 0.0 copy-start.1
  86.1 0.0 copy-start.2
  86.1 1.0 mul.771
  87.2 24.0 %all_gather.51 = f32[196,1024]{0,1:T(8,128)S(1)} all-gather(f32[196,64]{0,1:T(8,128)S(1)} %copy-done.4), channel_id=1, replica_groups=mesh['grp'=2,'spec'=16] {'spec'}, dimensions={1}, use_global_device_ids=true | all-gather | bytes 852992 | tf_op jit(solution)/shard_map/all_gather | solution.py:46
  111.2 0.3 copy.45
  111.5 1.0 mul.774
  112.5 0.6 dynamic-slice
  113.8 0.2 dynamic-update-slice
  114.0 0.2 dynamic-update-slice.1
  114.2 0.2 dynamic-update-slice.2
  114.5 0.2 dynamic-update-slice.3
  114.7 0.2 dynamic-update-slice.4
  114.9 64.3 %all-reduce.6 = (f32[1024]{0:T(1024)S(1)}, f32[1024]{0:T(1024)S(1)}, f32[1024]{0:T(1024)S(1)}, f32[1024]{0:T(1024)S(1)}, f32[1024]{0:T(1024)S(1)}) all-reduce(f32[1024]{0:T(1024)S(1)} %dynamic-update-slice, f32[1024]{0:T(1024)S(1)} %dynamic-update-slice.3, f32[1024]{0:T(1024)S(1)} %dynamic-update-slice.1, ...), channel_id=1, replica_groups=mesh['grp'=2,'spec'=16] {'spec'}, use_global_device_ids=true, to_apply=%add.1 | all-reduce | flops 5120 | bytes 40960
  179.2 1.1 fusion.114
  180.3 1.4 fusion.112
  181.7 1.3 fusion.113
  183.0 3.9 multiply_reduce_fusion.4
  186.9 0.0 all-gather.9.cloned.1.call-done
  187.0 5.1 %convert_bitcast_fusion.1 = f32[2,196,4096]{2,0,1:T(2,128)S(1)} fusion(bf16[4096,2,196]{0,1,2:T(2,128)(2,1)} %all-gather.9.cloned.1.call-done), kind=kLoop, calls=%fused_computation.61 | loop fusion | flops 1605632 | bytes 9633792 | tf_op jit(solution)/shard_map/transpose | solution.py:68
  192.0 6.5 %copy.38 = f32[2,196,4096]{2,1,0:T(8,128)} copy(f32[2,196,4096]{2,0,1:T(2,128)S(1)} %convert_bitcast_fusion.1) | data formatting | bytes 12845056 | tf_op jit(solution)/shard_map/transpose | solution.py:68
  198.5 5.8 %fusion.111 = (f32[1,196,4096]{2,0,1:T(1,128)S(1)}, f32[1,196,4096]{2,0,1:T(1,128)}) fusion(f32[2,196,4096]{2,0,1:T(2,128)S(1)} %convert_bitcast_fusion.1), kind=kLoop, calls=%fused_computation.179 | loop fusion | bytes 12845056 | tf_op jit(solution)/shard_map/slice | solution.py:75
  204.3 11.2 %pad_maximum_fusion = f32[2,196,4096]{2,0,1:T(2,128)} fusion(f32[1,196,4096]{2,0,1:T(1,128)} %get-tuple-element.27, f32[1,196,4096]{2,0,1:T(1,128)S(1)} %get-tuple-element.26), kind=kLoop, calls=%fused_computation.58 | loop fusion | flops 1605632 | bytes 12845056 | tf_op jit(solution)/shard_map/stack | solution.py:76
  215.5 9.3 %copy.39 = f32[2,196,4096]{2,1,0:T(8,128)} copy(f32[2,196,4096]{2,0,1:T(2,128)} %pad_maximum_fusion) | data formatting | bytes 12845056 | tf_op jit(solution)/shard_map/stack | solution.py:76
  224.8 5.5 %convert_bitcast_fusion = f32[2,196,4096]{2,0,1:T(2,128)S(1)} fusion(bf16[4096,2,196]{0,1,2:T(2,128)(2,1)} %all-gather.13.cloned.1.call-done), kind=kLoop, calls=%fused_computation.60 | loop fusion | flops 1605632 | bytes 9633792 | tf_op jit(solution)/shard_map/transpose | solution.py:73
  230.3 6.5 %copy.42 = f32[2,196,4096]{2,1,0:T(8,128)} copy(f32[2,196,4096]{2,0,1:T(2,128)S(1)} %convert_bitcast_fusion) | data formatting | bytes 12845056 | tf_op jit(solution)/shard_map/transpose | solution.py:73
  236.7 5.8 %fusion.110 = (f32[1,196,4096]{2,0,1:T(1,128)S(1)}, f32[1,196,4096]{2,0,1:T(1,128)}) fusion(f32[2,196,4096]{2,0,1:T(2,128)S(1)} %convert_bitcast_fusion), kind=kLoop, calls=%fused_computation.178 | loop fusion | bytes 12845056 | tf_op jit(solution)/shard_map/slice | solution.py:77
  242.5 11.2 %pad_maximum_fusion.1 = f32[2,196,4096]{2,0,1:T(2,128)} fusion(f32[1,196,4096]{2,0,1:T(1,128)} %get-tuple-element.25, f32[1,196,4096]{2,0,1:T(1,128)S(1)} %get-tuple-element.24), kind=kLoop, calls=%fused_computation.59 | loop fusion | flops 1605632 | bytes 12845056 | tf_op jit(solution)/shard_map/stack | solution.py:78
  253.6 9.3 %copy.43 = f32[2,196,4096]{2,1,0:T(8,128)} copy(f32[2,196,4096]{2,0,1:T(2,128)} %pad_maximum_fusion.1) | data formatting | bytes 12845056 | tf_op jit(solution)/shard_map/stack | solution.py:78
  262.9 22.9 %add_reduce_fusion = (f32[2,2]{1,0:T(2,128)S(1)}, f32[2,2,196,4096]{3,2,1,0:T(8,128)}) fusion(f32[4096]{0:T(1024)S(1)} %bitcast.98, f32[2,196,4096]{2,1,0:T(8,128)} %copy.43, f32[2,196,4096]{2,1,0:T(8,128)} %copy.42, f32[2,196,4096]{2,1,0:T(8,128)} %copy.39, f32[2,196,4096]{2,1,0:T(8,128)} %copy.38, bf16[4096,1024]{1,0:T(8,128)(2,1)} %all-gather.7.cloned.1.call-done, ...), kind=kOutput, calls=%fused_computation.48 | convolution fusion | flops 6611992576 | bytes 48545808 | tf_op jit(solution)/shard_map/dot_general | solution.py:62
  285.8 16.8 %multiply_reduce_fusion.1 = (f32[2,2]{1,0:T(2,128)S(1)}, f32[2,2,196]{2,1,0:T(2,128)S(1)}, f32[2,2,196,1024]{3,2,1,0:T(8,128)}) fusion(f32[1024]{0:T(1024)S(1)} %get-tuple-element.17, f32[1024]{0:T(1024)S(1)} %get-tuple-element.18, bf16[4096,1024]{1,0:T(8,128)(2,1)} %all-gather.11.cloned.1.call-done, f32[2,2,196,4096]{3,2,1,0:T(8,128)} %get-tuple-element.85, ...), kind=kOutput, calls=%fused_computation.63 | convolution fusion | flops 6599146496 | bytes 37301328 | tf_op jit(solution)/shard_map/dot_general | solution.py:90
  302.7 2.7 multiply_reduce_fusion
  305.4 2.0 reshape.145
  307.4 6.0 %copy.49 = f32[4,14,14,1024]{3,0,2,1:T(4,128)} copy(f32[4,14,14,1024]{3,2,1,0:T(8,128)} %reshape.145) | data formatting | bytes 6422528 | tf_op jit(solution)/shard_map/reshape | solution.py:104
  313.4 67.9 %multiply_reduce_fusion.3 = (f32[4]{0:T(128)S(1)}, f32[4]{0:T(128)S(1)}, f32[4,14,14,1024]{3,0,2,1:T(4,128)}) fusion(f32[14,14,1024]{2,1,0:T(8,128)} %mul.771, f32[4,14,14,1024]{3,0,2,1:T(4,128)S(1)} %copy-done, f32[14,14,1024]{2,1,0:T(8,128)} %mul.774, f32[1024]{0:T(1024)S(1)} %bitcast.112, f32[1024]{0:T(1024)S(1)} %bitcast.113, f32[1024]{0:T(1024)S(1)} %bitcast.114, ...), kind=kLoop, calls=%fused_computation.162 | loop fusion | flops 82690048 | bytes 11440160 | tf_op jit(solution)/shard_map/reduce_sum | solution.py:108
  381.4 0.1 negate_bitcast_fusion
  381.4 0.1 reduce_sum.71
  381.5 0.7 copy.46
  382.2 4.2 %reshape.111 = f32[2,2,196,1024]{3,1,0,2:T(2,128)S(1)} reshape(f32[4,14,14,1024]{3,0,2,1:T(4,128)} %get-tuple-element.23) | data formatting | bytes 6422528 | tf_op jit(solution)/shard_map/reshape | solution.py:104
  386.4 3.5 add_convert_fusion
  390.0 2.3 slice_bitcast_fusion
  (27 shorter events, 0.1 us)
Async XLA Ops:
  7.2 179.8 %all-gather.9.cloned.1.call-start = ((), (), s32[]{:S(2)}) async-start(), calls=%async_computation.1 | async-start | bytes 3411968 | tf_op jit(solution)/shard_map/all_gather | solution.py:68
  7.9 216.9 %all-gather.13.cloned.1.call-start = ((), (), s32[]{:S(2)}) async-start(), calls=%async_computation.3 | async-start | bytes 3411968 | tf_op jit(solution)/shard_map/all_gather | solution.py:71
  8.6 254.3 %all-gather.7.cloned.1.call-start = ((), (), s32[]{:S(2)}) async-start(), calls=%async_computation | async-start | bytes 8912896 | tf_op jit(solution)/shard_map/all_gather | solution.py:64
  9.4 276.4 %all-gather.11.cloned.1.call-start = ((), (), s32[]{:S(2)}) async-start(), calls=%async_computation.2 | async-start | bytes 8912896 | tf_op jit(solution)/shard_map/all_gather | solution.py:92
  58.8 4.0 %copy-start.3 = (f32[196,64]{0,1:T(8,128)S(1)}, f32[196,64]{0,1:T(8,128)}, u32[]{:S(2)}) copy-start(f32[196,64]{0,1:T(8,128)} %param.24) | copy-start | bytes 150532
  62.8 24.3 %copy-start.4 = (f32[196,64]{0,1:T(8,128)S(1)}, f32[196,64]{0,1:T(8,128)}, u32[]{:S(2)}) copy-start(f32[196,64]{0,1:T(8,128)} %param.25) | copy-start | bytes 150532
  86.0 26.5 %copy-start.11 = (u32[32]{0:T(128)S(1)}, u32[32]{0:T(128)}, u32[]{:S(2)}) copy-start(u32[32]{0:T(128)} %constant.14) | copy-start | bytes 388
  86.0 27.7 %copy-start.6 = (f32[64]{0:T(128)S(1)}, f32[64]{0:T(128)}, u32[]{:S(2)}) copy-start(f32[64]{0:T(128)} %param.30) | copy-start | bytes 772
  86.0 28.0 %copy-start.7 = (f32[64]{0:T(128)S(1)}, f32[64]{0:T(128)}, u32[]{:S(2)}) copy-start(f32[64]{0:T(128)} %param.28) | copy-start | bytes 772
  86.0 28.2 %copy-start.8 = (f32[64]{0:T(128)S(1)}, f32[64]{0:T(128)}, u32[]{:S(2)}) copy-start(f32[64]{0:T(128)} %param.31) | copy-start | bytes 772
  86.1 28.4 %copy-start.9 = (f32[64]{0:T(128)S(1)}, f32[64]{0:T(128)}, u32[]{:S(2)}) copy-start(f32[64]{0:T(128)} %param.29) | copy-start | bytes 772
  86.1 28.6 %copy-start.10 = (f32[64]{0:T(128)S(1)}, f32[64]{0:T(128)}, u32[]{:S(2)}) copy-start(f32[64]{0:T(128)} %param.27) | copy-start | bytes 772
  86.1 96.9 %copy-start.1 = (bf16[2,196,1024]{2,0,1:T(2,128)(2,1)S(1)}, bf16[2,196,1024]{2,0,1:T(2,128)(2,1)}, u32[]{:S(2)}) copy-start(bf16[2,196,1024]{2,0,1:T(2,128)(2,1)} %param.17) | copy-start | bytes 2408452
  86.1 96.9 %copy-start.2 = (bf16[2,196,1024]{2,0,1:T(2,128)(2,1)S(1)}, bf16[2,196,1024]{2,0,1:T(2,128)(2,1)}, u32[]{:S(2)}) copy-start(bf16[2,196,1024]{2,0,1:T(2,128)(2,1)} %param.16) | copy-start | bytes 2408452
  285.8 16.9 %copy-start.5 = (f32[196]{0:T(256)S(1)}, f32[196]{0:T(256)}, u32[]{:S(2)}) copy-start(f32[196]{0:T(256)} %param.23) | copy-start | bytes 2356
  307.4 6.0 %copy-start = (f32[4,14,14,1024]{3,0,2,1:T(4,128)S(1)}, f32[4,14,14,1024]{3,0,2,1:T(4,128)}, u32[]{:S(2)}) copy-start(f32[4,14,14,1024]{3,0,2,1:T(4,128)} %reshape.112) | copy-start | bytes 9633796
Sparse Core Ops, SparseCore 0:
  10.1 60.3 all-gather.8
  72.6 55.7 all-gather.12
  130.6 74.5 all-gather.6
  207.1 73.2 all-gather.10
where the time goes:
time: 405 us; the launch traced here: 399 us
  blocking collectives  155 us (38%)
  other arithmetic  114 us (28%)
  local copies, waits for them, and re-layouts  72.2 us (18%)
  matrix products  39.7 us (10%)
  between operations  14.9 us (4%)
    reduce_sum x1, other arithmetic, local(): linear = jnp.sum(total * center, axis=(2, 3))  67.9 us
    unnamed x1, blocking collectives  64.3 us
    all_gather x1, blocking collectives, local(): lax.all_gather(box_radius, 'spec', axis=1, tiled=True)  24 us
    all_gather x1, blocking collectives, local(): lax.all_gather(pw1_bias, 'spec', axis=0, tiled=True).astype(jnp.float32)  23.1 us
    dot_general x1, matrix products, local(): jnp.dot(flat, lax.all_gather(w_down, 'spec', axis=0, tiled=True).T, prefe...  22.9 us
    all_gather x1, blocking collectives, local(): lax.all_gather(box_center, 'spec', axis=1, tiled=True)  22.8 us
    all_gather x1, blocking collectives, local(): lax.all_gather(dw_weight, 'spec', axis=1, tiled=True)  21 us
    dot_general x1, matrix products, local(): jnp.dot(relaxed16, lax.all_gather(w_up, 'spec', axis=0, tiled=True), pref...  16.8 us
  transfers between devices with their start and end apart: 4, of which 0 were waited for; matrix products, arithmetic and copies ran while one was open for 30% of the time, Pallas kernels for 0%

commit v1 on v0

--- a/solution.py
+++ b/solution.py
@@ -1,3 +1,5 @@
+import functools
+
 import jax
 import jax.numpy as jnp
 from jax import lax
@@ -24,6 +26,7 @@
 
 
 def local(
+    nsh,
     lower_coef,
     upper_coef,
     w_down,
@@ -41,19 +44,52 @@
     ls_gamma,
     pw2_bias,
 ):
-    center, radius, kernel_taps, conv_bias, gain, norm_bias, gamma, out_bias = (
-        lax.all_gather(box_center, "spec", axis=1, tiled=True),
-        lax.all_gather(box_radius, "spec", axis=1, tiled=True),
-        lax.all_gather(dw_weight, "spec", axis=1, tiled=True),
-        lax.all_gather(dw_bias, "spec", axis=0, tiled=True),
-        lax.all_gather(ln_gain, "spec", axis=0, tiled=True),
-        lax.all_gather(ln_bias, "spec", axis=0, tiled=True),
-        lax.all_gather(ls_gamma, "spec", axis=0, tiled=True),
-        lax.all_gather(pw2_bias, "spec", axis=0, tiled=True),
+    nrows, npix, chans = lower_coef.shape
+    hl = w_down.shape[0]
+    cl = dw_bias.shape[0]
+    ntap = dw_weight.shape[0]
+
+    small = jnp.concatenate(
+        [
+            box_center,
+            box_radius,
+            dw_weight,
+            dw_bias[None],
+            ln_gain[None],
+            ln_bias[None],
+            ls_gamma[None],
+            pw2_bias[None],
+        ],
+        axis=0,
     )
-    nrows = lower_coef.shape[0]
-    npix = lower_coef.shape[1]
-    chans = lower_coef.shape[2]
+    nsmall = small.shape[0]
+    small_g = lax.all_gather(small, "spec", axis=0, tiled=False)
+    small_full = small_g.transpose(1, 0, 2).reshape(nsmall, nsh * cl)
+    o = 0
+    center = small_full[o : o + npix]
+    o += npix
+    radius = small_full[o : o + npix]
+    o += npix
+    kernel_taps = small_full[o : o + ntap]
+    o += ntap
+    conv_bias, gain, norm_bias, gamma, out_bias = (small_full[o + i] for i in range(5))
+
+    relax = jnp.concatenate(
+        [
+            slopes.transpose(1, 2, 0).reshape(2 * npix, hl),
+            intercepts.transpose(1, 2, 0).reshape(2 * npix, hl),
+            pw1_bias[None],
+        ],
+        axis=0,
+    )
+    relax_g = lax.all_gather(relax, "spec", axis=0, tiled=False).astype(jnp.float32)
+
+    def relax_map(i):
+        return relax_g[:, i * npix : (i + 1) * npix].transpose(1, 0, 2)
+
+    s0, s1, c0, c1 = (relax_map(i) for i in range(4))
+    hid_bias = relax_g[:, 4 * npix]
+
     height = 2 * nrows * npix
     coef = jnp.stack([lower_coef, upper_coef]).astype(jnp.float32)
     scaled = coef * gamma
@@ -63,36 +99,23 @@
         flat,
         lax.all_gather(w_down, "spec", axis=0, tiled=True).T,
         preferred_element_type=jnp.float32,
-    ).reshape(2, nrows, npix, -1)
-    slope_f = (
-        lax.all_gather(slopes, "spec", axis=0, tiled=True).astype(jnp.float32).transpose(1, 2, 0)
-    )
-    icpt_f = (
-        lax.all_gather(intercepts, "spec", axis=0, tiled=True)
-        .astype(jnp.float32)
-        .transpose(1, 2, 0)
-    )
-    first = jnp.stack([slope_f[0], slope_f[1]])[:, None]
-    second = jnp.stack([slope_f[1], slope_f[0]])[:, None]
-    first_icpt = jnp.stack([icpt_f[0], icpt_f[1]])[:, None]
-    second_icpt = jnp.stack([icpt_f[1], icpt_f[0]])[:, None]
+    ).reshape(2, nrows, npix, nsh, hl)
+    first = jnp.stack([s0, s1])[:, None]
+    second = jnp.stack([s1, s0])[:, None]
+    first_icpt = jnp.stack([c0, c1])[:, None]
+    second_icpt = jnp.stack([c1, c0])[:, None]
     positive = jnp.maximum(hidden, 0.0)
     negative = jnp.minimum(hidden, 0.0)
     relaxed = positive * first + negative * second
     extra = jnp.sum(
-        positive * first_icpt
-        + negative * second_icpt
-        + relaxed * lax.all_gather(pw1_bias, "spec", axis=0, tiled=True).astype(jnp.float32),
-        axis=(2, 3),
+        positive * first_icpt + negative * second_icpt + relaxed * hid_bias,
+        axis=(2, 3, 4),
     )
-    relaxed16, extra = (relaxed.astype(jnp.bfloat16).reshape(height, -1), extra)
-    normed, extra = (
-        jnp.dot(
-            relaxed16,
-            lax.all_gather(w_up, "spec", axis=0, tiled=True),
-            preferred_element_type=jnp.float32,
-        ),
-        extra,
+    relaxed16 = relaxed.astype(jnp.bfloat16).reshape(height, -1)
+    normed = jnp.dot(
+        relaxed16,
+        lax.all_gather(w_up, "spec", axis=0, tiled=True),
+        preferred_element_type=jnp.float32,
     )
     bias = bias + extra
     normed = normed.reshape(2, nrows, npix, chans)
@@ -131,7 +154,7 @@
         P("spec"),
     )
     return jax.shard_map(
-        local,
+        functools.partial(local, mesh.shape["spec"]),
         mesh=mesh,
         in_specs=placed,
         out_specs=(

time: 405 us -> 381 us (0.941); the launches traced: 399 us -> 380 us
  blocking collectives: 155 us -> 0 us
  waiting for transfers between devices: 2.61 us -> 156 us
  matrix products: 39.7 us -> 31.2 us
  other arithmetic: 114 us -> 108 us
    all_gather x4 -> x0, blocking collectives: 91 us -> none  [the longest x1 24 us: local(): lax.all_gather(box_radius, 'spec', axis=1, tiled=True)]
    all_gather x2, waiting for transfers between devices: 0.02 us -> 73.4 us  [the longest x1 41.2 us: local(): lax.all_gather(relax, 'spec', axis=0, tiled=False).astype(jnp.float32)]
    unnamed x1 -> x0, blocking collectives: 64.3 us -> none
    all_gather x1, waiting for transfers between devices: 0.01 us -> 41.3 us  [local(): lax.all_gather(w_up, 'spec', axis=0, tiled=True)]
    all_gather x1, waiting for transfers between devices: 0.01 us -> 39.9 us  [local(): lax.all_gather(w_down, 'spec', axis=0, tiled=True)]
    transpose x2, local copies, waits for them, and re-layouts: 12.9 us -> 1.91 us  [the longest x1 0.95 us: local(): slopes.transpose(1, 2, 0).reshape(2 * npix, hl)]
    transpose x2 -> x0, other arithmetic: 10.5 us -> none  [the longest x1 5.47 us: local(): icpt_f = lax.all_gather(intercepts, 'spec', axis=0, tiled=True).astype(jn...]
    another operation x2 -> x1, local copies, waits for them, and re-layouts: 18.6 us -> 8.88 us  [local(): first_icpt = jnp.stack([c0, c1])[:, None]]
  transfers between devices with their start and end apart: 4 -> 4, of which waited for: 0 -> 4; matrix products, arithmetic and copies ran while one was open for 30% -> 27% of each run, Pallas kernels for 0% -> 0%
where the time goes in v1:
time: 381 us; the launch traced here: 380 us
  waiting for transfers between devices  156 us (41%)
  other arithmetic  108 us (28%)
  local copies, waits for them, and re-layouts  70.2 us (18%)
  matrix products  31.2 us (8%)
  between operations  14.2 us (4%)
    reduce_sum x1, other arithmetic, local(): linear = jnp.sum(total * center, axis=(2, 3))  68.3 us
    all_gather x1, waiting for transfers between devices, local(): lax.all_gather(w_up, 'spec', axis=0, tiled=True)  41.3 us
    all_gather x1, waiting for transfers between devices, local(): lax.all_gather(relax, 'spec', axis=0, tiled=False).astype(jnp.float32)  41.2 us
    all_gather x1, waiting for transfers between devices, local(): lax.all_gather(w_down, 'spec', axis=0, tiled=True)  39.9 us
    all_gather x1, waiting for transfers between devices, local(): small_g = lax.all_gather(small, 'spec', axis=0, tiled=False)  32.2 us
    dot_general x1, matrix products, local(): jnp.dot(flat, lax.all_gather(w_down, 'spec', axis=0, tiled=True).T, prefe...  19.5 us
    another operation x1, other arithmetic, local(): first = jnp.stack([s0, s1])[:, None]  17.4 us
    dot_general x1, matrix products, local(): jnp.dot(relaxed16, lax.all_gather(w_up, 'spec', axis=0, tiled=True), pref...  11.7 us
  transfers between devices with their start and end apart: 4, of which 4 were waited for; matrix products, arithmetic and copies ran while one was open for 27% of the time, Pallas kernels for 0%

profile of v1, /device:TPU:0, one launch (start us, length us, event | category | flops | bytes accessed | tf_op | source)
XLA Modules:
  0.0 379.8 jit_solution(5004694763646667036)
XLA Ops:
  7.2 0.0 all-gather.13.cloned.1.call-start
  7.2 0.8 copy.48
  8.0 0.7 copy.49
  8.8 0.7 copy.50
  9.5 0.7 copy.51
  10.3 0.7 copy.52
  11.0 0.7 copy.53
  11.8 1.7 concatenate.6
  13.4 0.0 all-gather.13.cloned.1.call-update
  13.4 0.0 all-gather.15.cloned.1.call-start
  13.5 1.0 copy.55
  14.5 1.0 copy.56
  15.5 0.7 broadcast_in_dim.31
  16.2 0.8 maximum_bitcast_fusion
  17.0 0.0 all-gather.15.cloned.1.call-update
  17.0 0.0 all-gather.9.cloned.1.call-start
  17.0 0.7 all-gather.9.cloned.1.call-update
  17.7 0.0 all-gather.11.cloned.1.call-start
  17.8 0.5 all-gather.11.cloned.1.call-update
  18.3 3.1 fusion.103
  21.4 4.1 %reshape.138 = f32[4,14,14,1024]{3,0,2,1:T(4,128)} reshape(f32[2,2,196,1024]{3,1,0,2:T(2,128)S(1)} %fusion.103) | data formatting | bytes 6422528 | tf_op jit(solution)/shard_map/convert_element_type | solution.py:94
  25.5 32.2 %all-gather.13.cloned.1.call-done = f32[16,446,64]{1,2,0:T(8,128)} async-done(((f32[1,446,64]{1,2,0:T(8,128)}), f32[16,446,64]{1,2,0:T(8,128)}) %all-gather.13.cloned.1.call-update) | async-done | bytes 1826832 | tf_op jit(solution)/shard_map/all_gather | solution.py:66
  57.7 1.4 slice.476
  59.1 3.7 slice_reduce_fusion.2
  62.8 0.7 mul.615
  63.4 0.7 mul.773
  64.1 0.7 mul.622
  64.8 0.7 mul.783
  65.4 0.7 mul.786
  66.1 0.3 copy.59
  66.3 0.2 reshape.136
  66.5 0.0 copy-done
  66.5 1.4 fusion.105
  67.9 1.1 copy.60
  69.0 1.4 mul.789
  70.4 2.4 copy.61
  72.8 1.4 mul.792
  74.3 0.7 fusion.106
  74.9 0.7 fusion.107
  75.6 5.4 %multiply_reduce_fusion.4 = (f32[2,2]{1,0:T(2,128)S(1)}, bf16[2,2,196,1024,1]{3,1,0,2,4:T(2,128)(2,1)}) fusion(f32[1024]{0:T(1024)} %mul.773, f32[1024]{0:T(1024)} %mul.615, bf16[1,2,196,1024]{3,1,0,2:T(2,128)(2,1)S(1)} %bitcast.119, bf16[1,2,196,1024]{3,1,0,2:T(2,128)(2,1)S(1)} %bitcast.122), kind=kLoop, calls=%fused_computation.162 | loop fusion | flops 4816892 | bytes 3219472 | tf_op jit(solution)/shard_map/reduce_sum | solution.py:96
  81.0 41.2 %all-gather.15.cloned.1.call-done = bf16[16,785,256]{2,1,0:T(8,128)(2,1)} async-done(((bf16[1,785,256]{2,1,0:T(8,128)(2,1)}), bf16[16,785,256]{2,1,0:T(8,128)(2,1)}) %all-gather.15.cloned.1.call-update) | async-done | bytes 6430736 | tf_op jit(solution)/shard_map/all_gather | solution.py:85
  122.3 0.8 slice.531
  123.1 8.7 %convert_element_type.43 = f32[16,785,256]{2,1,0:T(8,128)} convert(bf16[16,785,256]{2,1,0:T(8,128)(2,1)} %all-gather.15.cloned.1.call-done) | non-fusion elementwise | flops 3215360 | bytes 19292160 | tf_op jit(solution)/shard_map/convert_element_type | solution.py:85
  131.8 8.9 %slice_bitcast_fusion = (f32[1,196,16,256]{3,1,2,0:T(8,128)S(1)}, f32[1,196,16,256]{3,1,2,0:T(8,128)}, f32[1,196,16,256]{3,1,2,0:T(8,128)}, f32[1,196,16,256]{3,1,2,0:T(8,128)}) fusion(f32[16,785,256]{2,1,0:T(8,128)} %convert_element_type.43), kind=kLoop, calls=%fused_computation.57 | loop fusion | bytes 25690112 | tf_op jit(solution)/shard_map/stack | solution.py:105
  140.7 17.4 %pad_maximum_fusion = (f32[2,196,16,256]{3,1,2,0:T(8,128)}, f32[2,196,16,256]{3,1,2,0:T(8,128)}, f32[2,196,16,256]{3,1,2,0:T(8,128)}, f32[2,196,16,256]{3,1,2,0:T(8,128)}) fusion(f32[1,196,16,256]{3,1,2,0:T(8,128)} %get-tuple-element.28, f32[1,196,16,256]{3,1,2,0:T(8,128)} %get-tuple-element.29, f32[1,196,16,256]{3,1,2,0:T(8,128)} %get-tuple-element.27, ...), kind=kLoop, calls=%fused_computation.53 | loop fusion | flops 6422528 | bytes 38535168 | tf_op jit(solution)/shard_map/stack | solution.py:103
  158.1 39.9 %all-gather.9.cloned.1.call-done = bf16[4096,1024]{1,0:T(8,128)(2,1)} async-done(((bf16[256,1024]{1,0:T(8,128)(2,1)}), bf16[4096,1024]{1,0:T(8,128)(2,1)}) %all-gather.9.cloned.1.call-update) | async-done | bytes 8388624 | tf_op jit(solution)/shard_map/all_gather | solution.py:100
  198.0 19.5 %add_reduce_fusion = (f32[2,2]{1,0:T(2,128)S(1)}, bf16[2,2,196,16,256]{4,2,3,1,0:T(8,128)(2,1)}) fusion(f32[16,256]{1,0:T(8,128)S(1)} %bitcast.123, f32[2,196,16,256]{3,1,2,0:T(8,128)} %get-tuple-element.92, f32[2,196,16,256]{3,1,2,0:T(8,128)} %get-tuple-element.93, f32[2,196,16,256]{3,1,2,0:T(8,128)} %get-tuple-element.33, ...), kind=kOutput, calls=%fused_computation.48 | convolution fusion | flops 6615203840 | bytes 42123280 | tf_op jit(solution)/shard_map/dot_general | solution.py:98
  217.5 6.8 %copy.57 = bf16[2,2,196,16,256]{4,3,2,1,0:T(8,128)(2,1)} copy(bf16[2,2,196,16,256]{4,2,3,1,0:T(8,128)(2,1)} %get-tuple-element.25) | data formatting | bytes 12845056 | tf_op jit(solution)/shard_map/convert_element_type | solution.py:114
  224.3 7.5 %dot_general.12 = bf16[2,2,196,4096]{3,2,1,0:T(8,128)(2,1)} reshape(bf16[2,2,196,16,256]{4,3,2,1,0:T(8,128)(2,1)} %copy.57) | data formatting | bytes 12845056 | tf_op jit(solution)/shard_map/dot_general | solution.py:115
  231.8 41.3 %all-gather.11.cloned.1.call-done = bf16[4096,1024]{1,0:T(8,128)(2,1)} async-done(((bf16[256,1024]{1,0:T(8,128)(2,1)}), bf16[4096,1024]{1,0:T(8,128)(2,1)}) %all-gather.11.cloned.1.call-update) | async-done | bytes 8388624 | tf_op jit(solution)/shard_map/all_gather | solution.py:117
  273.2 11.7 %multiply_reduce_fusion.1 = (f32[2,2]{1,0:T(2,128)S(1)}, f32[2,2,196]{2,1,0:T(2,128)S(1)}, f32[2,2,196,1024]{3,2,1,0:T(8,128)S(1)}) fusion(f32[1024]{0:T(1024)S(1)} %copy-done.27, f32[1024]{0:T(1024)S(1)} %copy-done.25, bf16[2,2,196,4096]{3,2,1,0:T(8,128)(2,1)} %dot_general.12, bf16[4096,1024]{1,0:T(8,128)(2,1)} %all-gather.11.cloned.1.call-done), kind=kOutput, calls=%fused_computation.62 | convolution fusion | flops 6579878912 | bytes 18033744 | tf_op jit(solution)/shard_map/dot_general | solution.py:115
  284.9 0.0 copy-done.26
  284.9 0.0 copy-done.28
  284.9 0.9 multiply_reduce_fusion
  285.8 2.0 reshape.152
  288.0 6.0 %copy.68 = f32[4,14,14,1024]{3,0,2,1:T(4,128)} copy(f32[4,14,14,1024]{3,2,1,0:T(8,128)} %reshape.152) | data formatting | bytes 6422528 | tf_op jit(solution)/shard_map/reshape | solution.py:127
  293.9 0.0 copy-done.4
  294.1 68.3 %multiply_reduce_fusion.3 = (f32[4]{0:T(128)S(1)}, f32[4]{0:T(128)S(1)}, f32[4,14,14,1024]{3,0,2,1:T(4,128)}) fusion(f32[14,14,1024]{2,1,0:T(8,128)} %mul.789, f32[4,14,14,1024]{3,0,2,1:T(4,128)S(1)} %copy-done.1, f32[14,14,1024]{2,1,0:T(8,128)} %mul.792, f32[1024]{0:T(1024)S(1)} %bitcast.139, f32[1024]{0:T(1024)S(1)} %bitcast.140, f32[1024]{0:T(1024)S(1)} %bitcast.141, ...), kind=kLoop, calls=%fused_computation.161 | loop fusion | flops 82690048 | bytes 11440160 | tf_op jit(solution)/shard_map/reduce_sum | solution.py:131
  362.4 0.1 negate_bitcast_fusion
  362.5 0.1 reduce_sum.71
  362.6 0.7 copy.62
  363.2 4.2 %reshape.137 = f32[2,2,196,1024]{3,1,0,2:T(2,128)S(1)} reshape(f32[4,14,14,1024]{3,0,2,1:T(4,128)} %get-tuple-element.23) | data formatting | bytes 6422528 | tf_op jit(solution)/shard_map/reshape | solution.py:127
  367.4 3.5 add_convert_fusion
  371.0 2.3 slice_bitcast_fusion.4
  (60 shorter events, 0.2 us)
Async XLA Ops:
  7.2 50.5 %all-gather.13.cloned.1.call-start = ((), (), s32[]{:S(2)}) async-start(), calls=%async_computation.2 | async-start | bytes 2228224 | tf_op jit(solution)/shard_map/all_gather | solution.py:66
  13.4 108.8 %all-gather.15.cloned.1.call-start = ((), (), s32[]{:S(2)}) async-start(), calls=%async_computation.3 | async-start | bytes 6893568 | tf_op jit(solution)/shard_map/all_gather | solution.py:85
  17.0 181.0 %all-gather.9.cloned.1.call-start = ((), (), s32[]{:S(2)}) async-start(), calls=%async_computation | async-start | bytes 8912896 | tf_op jit(solution)/shard_map/all_gather | solution.py:100
  17.7 255.4 %all-gather.11.cloned.1.call-start = ((), (), s32[]{:S(2)}) async-start(), calls=%async_computation.1 | async-start | bytes 8912896 | tf_op jit(solution)/shard_map/all_gather | solution.py:117
  57.7 8.8 %copy-start = (f32[16,446,64]{1,2,0:T(8,128)S(1)}, f32[16,446,64]{1,2,0:T(8,128)}, u32[]{:S(2)}) copy-start(f32[16,446,64]{1,2,0:T(8,128)} %all-gather.13.cloned.1.call-done) | copy-start | bytes 5480452
  70.4 5.3 %copy-start.2 = (bf16[2,196,1024]{2,0,1:T(2,128)(2,1)S(1)}, bf16[2,196,1024]{2,0,1:T(2,128)(2,1)}, u32[]{:S(2)}) copy-start(bf16[2,196,1024]{2,0,1:T(2,128)(2,1)} %param.17) | copy-start | bytes 2408452
  70.4 5.3 %copy-start.3 = (bf16[2,196,1024]{2,0,1:T(2,128)(2,1)S(1)}, bf16[2,196,1024]{2,0,1:T(2,128)(2,1)}, u32[]{:S(2)}) copy-start(bf16[2,196,1024]{2,0,1:T(2,128)(2,1)} %param.16) | copy-start | bytes 2408452
  224.3 48.8 %copy-start.25 = (f32[1024]{0:T(1024)S(1)}, f32[1024]{0:T(1024)}, u32[]{:S(2)}) copy-start(f32[1024]{0:T(1024)} %mul.622) | copy-start | bytes 12292
  224.3 48.8 %copy-start.27 = (f32[1024]{0:T(1024)S(1)}, f32[1024]{0:T(1024)}, u32[]{:S(2)}) copy-start(f32[1024]{0:T(1024)} %mul.783) | copy-start | bytes 12292
  231.8 53.1 %copy-start.26 = (f32[1024]{0:T(1024)S(1)}, f32[1024]{0:T(1024)}, u32[]{:S(2)}) copy-start(f32[1024]{0:T(1024)} %mul.786) | copy-start | bytes 12292
  231.8 53.1 %copy-start.28 = (f32[196]{0:T(256)S(1)}, f32[196]{0:T(256)}, u32[]{:S(2)}) copy-start(f32[196]{0:T(256)} %param.23) | copy-start | bytes 2356
  287.8 6.2 %copy-start.1 = (f32[4,14,14,1024]{3,0,2,1:T(4,128)S(1)}, f32[4,14,14,1024]{3,0,2,1:T(4,128)}, u32[]{:S(2)}) copy-start(f32[4,14,14,1024]{3,0,2,1:T(4,128)} %reshape.138) | copy-start | bytes 9633796
  287.8 6.2 %copy-start.4 = (f32[1,1,1024]{2,1,0:T(1,128)S(1)}, f32[1,1,1024]{2,1,0:T(1,128)}, u32[]{:S(2)}) copy-start(f32[1,1,1024]{2,1,0:T(1,128)} %get-tuple-element.57) | copy-start | bytes 12292
  287.8 6.2 %copy-start.5 = (f32[1,1,1024]{2,1,0:T(1,128)S(1)}, f32[1,1,1024]{2,1,0:T(1,128)}, u32[]{:S(2)}) copy-start(f32[1,1,1024]{2,1,0:T(1,128)} %get-tuple-element.58) | copy-start | bytes 12292
  287.8 6.2 %copy-start.6 = (f32[1,1,1024]{2,1,0:T(1,128)S(1)}, f32[1,1,1024]{2,1,0:T(1,128)}, u32[]{:S(2)}) copy-start(f32[1,1,1024]{2,1,0:T(1,128)} %get-tuple-element.59) | copy-start | bytes 12292
  287.8 6.2 %copy-start.7 = (f32[1,1,1024]{2,1,0:T(1,128)S(1)}, f32[1,1,1024]{2,1,0:T(1,128)}, u32[]{:S(2)}) copy-start(f32[1,1,1024]{2,1,0:T(1,128)} %get-tuple-element.60) | copy-start | bytes 12292
  287.8 6.2 %copy-start.8 = (f32[1,1,1024]{2,1,0:T(1,128)S(1)}, f32[1,1,1024]{2,1,0:T(1,128)}, u32[]{:S(2)}) copy-start(f32[1,1,1024]{2,1,0:T(1,128)} %get-tuple-element.61) | copy-start | bytes 12292
  287.8 6.2 %copy-start.9 = (f32[1,1,1024]{2,1,0:T(1,128)S(1)}, f32[1,1,1024]{2,1,0:T(1,128)}, u32[]{:S(2)}) copy-start(f32[1,1,1024]{2,1,0:T(1,128)} %get-tuple-element.62) | copy-start | bytes 12292
  287.8 6.2 %copy-start.10 = (f32[1,1,1024]{2,1,0:T(1,128)S(1)}, f32[1,1,1024]{2,1,0:T(1,128)}, u32[]{:S(2)}) copy-start(f32[1,1,1024]{2,1,0:T(1,128)} %get-tuple-element.63) | copy-start | bytes 12292
  287.8 6.2 %copy-start.11 = (f32[1,1,1024]{2,1,0:T(1,128)S(1)}, f32[1,1,1024]{2,1,0:T(1,128)}, u32[]{:S(2)}) copy-start(f32[1,1,1024]{2,1,0:T(1,128)} %get-tuple-element.64) | copy-start | bytes 12292
  287.8 6.2 %copy-start.12 = (f32[1,1,1024]{2,1,0:T(1,128)S(1)}, f32[1,1,1024]{2,1,0:T(1,128)}, u32[]{:S(2)}) copy-start(f32[1,1,1024]{2,1,0:T(1,128)} %get-tuple-element.65) | copy-start | bytes 12292
  287.9 6.2 %copy-start.13 = (f32[1,1,1024]{2,1,0:T(1,128)S(1)}, f32[1,1,1024]{2,1,0:T(1,128)}, u32[]{:S(2)}) copy-start(f32[1,1,1024]{2,1,0:T(1,128)} %get-tuple-element.66) | copy-start | bytes 12292
  287.9 6.2 %copy-start.14 = (f32[1,1,1024]{2,1,0:T(1,128)S(1)}, f32[1,1,1024]{2,1,0:T(1,128)}, u32[]{:S(2)}) copy-start(f32[1,1,1024]{2,1,0:T(1,128)} %get-tuple-element.67) | copy-start | bytes 12292
  287.9 6.2 %copy-start.15 = (f32[1,1,1024]{2,1,0:T(1,128)S(1)}, f32[1,1,1024]{2,1,0:T(1,128)}, u32[]{:S(2)}) copy-start(f32[1,1,1024]{2,1,0:T(1,128)} %get-tuple-element.68) | copy-start | bytes 12292
  287.9 6.2 %copy-start.16 = (f32[1,1,1024]{2,1,0:T(1,128)S(1)}, f32[1,1,1024]{2,1,0:T(1,128)}, u32[]{:S(2)}) copy-start(f32[1,1,1024]{2,1,0:T(1,128)} %get-tuple-element.69) | copy-start | bytes 12292
  287.9 6.2 %copy-start.17 = (f32[1,1,1024]{2,1,0:T(1,128)S(1)}, f32[1,1,1024]{2,1,0:T(1,128)}, u32[]{:S(2)}) copy-start(f32[1,1,1024]{2,1,0:T(1,128)} %get-tuple-element.70) | copy-start | bytes 12292
  287.9 6.2 %copy-start.18 = (f32[1,1,1024]{2,1,0:T(1,128)S(1)}, f32[1,1,1024]{2,1,0:T(1,128)}, u32[]{:S(2)}) copy-start(f32[1,1,1024]{2,1,0:T(1,128)} %get-tuple-element.71) | copy-start | bytes 12292
  287.9 6.2 %copy-start.19 = (f32[1,1,1024]{2,1,0:T(1,128)S(1)}, f32[1,1,1024]{2,1,0:T(1,128)}, u32[]{:S(2)}) copy-start(f32[1,1,1024]{2,1,0:T(1,128)} %get-tuple-element.72) | copy-start | bytes 12292
  287.9 6.2 %copy-start.20 = (f32[1,1,1024]{2,1,0:T(1,128)S(1)}, f32[1,1,1024]{2,1,0:T(1,128)}, u32[]{:S(2)}) copy-start(f32[1,1,1024]{2,1,0:T(1,128)} %get-tuple-element.73) | copy-start | bytes 12292
  287.9 6.2 %copy-start.21 = (f32[1,1,1024]{2,1,0:T(1,128)S(1)}, f32[1,1,1024]{2,1,0:T(1,128)}, u32[]{:S(2)}) copy-start(f32[1,1,1024]{2,1,0:T(1,128)} %get-tuple-element.74) | copy-start | bytes 12292
  287.9 6.2 %copy-start.22 = (f32[1,1,1024]{2,1,0:T(1,128)S(1)}, f32[1,1,1024]{2,1,0:T(1,128)}, u32[]{:S(2)}) copy-start(f32[1,1,1024]{2,1,0:T(1,128)} %get-tuple-element.75) | copy-start | bytes 12292
  288.0 6.2 %copy-start.23 = (f32[1,1,1024]{2,1,0:T(1,128)S(1)}, f32[1,1,1024]{2,1,0:T(1,128)}, u32[]{:S(2)}) copy-start(f32[1,1,1024]{2,1,0:T(1,128)} %get-tuple-element.76) | copy-start | bytes 12292
  288.0 6.2 %copy-start.24 = (f32[1,1,1024]{2,1,0:T(1,128)S(1)}, f32[1,1,1024]{2,1,0:T(1,128)}, u32[]{:S(2)}) copy-start(f32[1,1,1024]{2,1,0:T(1,128)} %get-tuple-element.77) | copy-start | bytes 12292
Sparse Core Ops, SparseCore 0:
  13.6 44.0 all-gather.12
  60.4 61.7 all-gather.14
  124.4 73.4 all-gather.8
  200.0 73.1 all-gather.10

commit v2 on v1

--- a/solution.py
+++ b/solution.py
@@ -51,8 +51,6 @@
 
     small = jnp.concatenate(
         [
-            box_center,
-            box_radius,
             dw_weight,
             dw_bias[None],
             ln_gain[None],
@@ -65,14 +63,8 @@
     nsmall = small.shape[0]
     small_g = lax.all_gather(small, "spec", axis=0, tiled=False)
     small_full = small_g.transpose(1, 0, 2).reshape(nsmall, nsh * cl)
-    o = 0
-    center = small_full[o : o + npix]
-    o += npix
-    radius = small_full[o : o + npix]
-    o += npix
-    kernel_taps = small_full[o : o + ntap]
-    o += ntap
-    conv_bias, gain, norm_bias, gamma, out_bias = (small_full[o + i] for i in range(5))
+    kernel_taps = small_full[:ntap]
+    conv_bias, gain, norm_bias, gamma, out_bias = (small_full[ntap + i] for i in range(5))
 
     relax = jnp.concatenate(
         [
@@ -123,11 +115,23 @@
     tilted = normed * gain
     centered = ln_scale[None, None, :, None] * (tilted - jnp.mean(tilted, axis=-1, keepdims=True))
     bias = bias + jnp.sum(centered * conv_bias, axis=(2, 3))
-    taps = kernel_taps.reshape(KERNEL, KERNEL, chans)
-    conv = conv_back(centered.reshape(2 * nrows, MAP, MAP, chans), taps).reshape(
-        2, nrows, npix, chans
-    )
+    taps = kernel_taps.reshape(KERNEL, KERNEL, 1, chans)[::-1, ::-1]
+    half = KERNEL // 2
+    conv = lax.conv_general_dilated(
+        centered.reshape(2 * nrows, MAP, MAP, chans),
+        taps,
+        window_strides=(1, 1),
+        padding=((half, half), (half, half)),
+        dimension_numbers=("NHWC", "HWIO", "NHWC"),
+        feature_group_count=chans,
+        precision=lax.Precision.HIGHEST,
+    ).reshape(2, nrows, npix, chans)
     total = coef + conv
+    box = jnp.stack([box_center, box_radius])
+    box, _ = lax.optimization_barrier((box, normed))
+    box_g = lax.all_gather(box, "spec", axis=0, tiled=False)
+    box_full = box_g.transpose(1, 2, 0, 3).reshape(2, npix, nsh * cl)
+    center, radius = box_full[0], box_full[1]
     linear = jnp.sum(total * center, axis=(2, 3))
     spread = jnp.sum(jnp.abs(total) * radius, axis=(2, 3))
     bounds = bias + linear + jnp.stack([-spread[0], spread[1]])

time: 381 us -> 328 us (0.86)
  other arithmetic: 108 us -> 40.3 us
  blocking collectives: 0 us -> 25.4 us
  matrix products: 31.2 us -> 49.5 us
  local copies, waits for them, and re-layouts: 70.2 us -> 55.5 us
  waiting for transfers between devices: 156 us -> 143 us
    reduce_sum x1 -> x0, other arithmetic: 68.3 us -> none  [local(): linear = jnp.sum(total * center, axis=(2, 3))]
    all_gather x0 -> x1, blocking collectives: none -> 25.4 us  [local(): small_g = lax.all_gather(small, 'spec', axis=0, tiled=False)]
    conv_general_dilated x0 -> x1, matrix products: none -> 17.8 us  [local(): lax.conv_general_dilated(centered.reshape(2 * nrows, MAP, MAP, chans), ta...]
    slice x9 -> x3, local copies, waits for them, and re-layouts: 11.6 us -> 3.1 us  [the longest x1 1.88 us: local(): center, radius = (box_full[0], box_full[1])]
    all_gather x1, waiting for transfers between devices: 41.2 us -> 33.7 us  [local(): lax.all_gather(relax, 'spec', axis=0, tiled=False).astype(jnp.float32)]
    all_gather x1, waiting for transfers between devices: 32.2 us -> 25.7 us  [local(): box_g = lax.all_gather(box, 'spec', axis=0, tiled=False)]
    reshape x2 -> x1, local copies, waits for them, and re-layouts: 7.97 us -> 2 us  [local(): centered.reshape(2 * nrows, MAP, MAP, chans)]
where the time goes in v2:
time: 328 us
  waiting for transfers between devices  143 us (44%)
  local copies, waits for them, and re-layouts  55.5 us (17%)
  matrix products  49.5 us (15%)
  other arithmetic  40.3 us (12%)
  blocking collectives  25.4 us (8%)
  between operations  14 us (4%)
    all_gather x1, waiting for transfers between devices, local(): lax.all_gather(w_up, 'spec', axis=0, tiled=True)  42.1 us
    all_gather x1, waiting for transfers between devices, local(): lax.all_gather(w_down, 'spec', axis=0, tiled=True)  39.8 us
    all_gather x1, waiting for transfers between devices, local(): lax.all_gather(relax, 'spec', axis=0, tiled=False).astype(jnp.float32)  33.7 us
    all_gather x1, waiting for transfers between devices, local(): box_g = lax.all_gather(box, 'spec', axis=0, tiled=False)  25.7 us
    all_gather x1, blocking collectives, local(): small_g = lax.all_gather(small, 'spec', axis=0, tiled=False)  25.4 us
    dot_general x1, matrix products, local(): jnp.dot(flat, lax.all_gather(w_down, 'spec', axis=0, tiled=True).T, prefe...  19 us
    conv_general_dilated x1, matrix products, local(): lax.conv_general_dilated(centered.reshape(2 * nrows, MAP, MAP, chans), ta...  17.8 us
    another operation x1, other arithmetic, local(): first = jnp.stack([s0, s1])[:, None]  17.3 us
  transfers between devices with their start and end apart: 4, of which 4 were waited for; matrix products, arithmetic and copies ran while one was open for 27% of the time, Pallas kernels for 0%

profile of v2, /device:TPU:0, one launch (start us, length us, event | category | flops | bytes accessed | tf_op | source)
XLA Modules:
  0.0 327.7 jit_solution(10689609590194245441)
XLA Ops:
  7.2 0.0 copy-start.8
  7.2 0.0 copy-start.10
  7.2 0.0 copy-start.11
  7.2 0.0 copy-start.12
  7.2 0.0 copy-start.13
  7.2 0.0 copy-start.14
  7.2 0.0 copy-start.6
  7.2 0.0 copy-start.7
  7.2 0.0 copy-start.1
  7.3 0.0 copy-start.3
  7.3 0.0 all-gather.16.cloned.1.call-start
  7.3 0.8 broadcast_in_dim.29
  8.1 0.9 copy.43
  9.1 1.0 copy.42
  10.1 0.8 maximum_bitcast_fusion
  10.9 0.0 all-gather.16.cloned.1.call-update
  10.9 0.0 all-gather.10.cloned.1.call-start
  11.0 0.7 all-gather.10.cloned.1.call-update
  11.7 0.0 all-gather.12.cloned.1.call-start
  11.7 0.7 all-gather.12.cloned.1.call-update
  12.4 0.0 all-gather.14.cloned.1.call-start
  12.5 25.4 %all-gather.3 = f32[16,54,64]{2,1,0:T(8,128)S(1)} all-gather(f32[1,54,64]{2,1,0:T(8,128)S(1)} %bitcast.88), channel_id=2, replica_groups=mesh['grp'=2,'spec'=16] {'spec'}, dimensions={0}, use_global_device_ids=true | all-gather | bytes 235008 | tf_op jit(solution)/shard_map/all_gather | solution.py:64
  38.0 0.8 copy-done.5
  38.7 0.1 slice_reduce_fusion.2
  38.9 0.1 mul.146
  38.9 0.1 mul.132
  39.0 0.1 mul.136
  39.1 0.1 mul.125
  39.2 0.7 pad_maximum_fusion.5
  39.8 0.0 copy-done.3
  39.8 4.5 %multiply_reduce_fusion.4 = (f32[2,2]{1,0:T(2,128)S(1)}, bf16[2,2,196,1024,1]{3,1,2,0,4:T(2,128)(2,1)}) fusion(f32[1024]{0:T(1024)S(1)} %mul.136, f32[1024]{0:T(1024)S(1)} %mul.125, bf16[1,2,196,1024]{3,1,2,0:T(2,128)(2,1)S(1)} %bitcast.77, bf16[1,2,196,1024]{3,1,2,0:T(2,128)(2,1)S(1)} %bitcast.80), kind=kLoop, calls=%fused_computation.22 | loop fusion | flops 4816892 | bytes 3219472 | tf_op jit(solution)/shard_map/reduce_sum | solution.py:88
  44.4 33.7 %all-gather.16.cloned.1.call-done = bf16[16,785,256]{2,1,0:T(8,128)(2,1)} async-done(((bf16[1,785,256]{2,1,0:T(8,128)(2,1)}), bf16[16,785,256]{2,1,0:T(8,128)(2,1)}) %all-gather.16.cloned.1.call-update) | async-done | bytes 6430736 | tf_op jit(solution)/shard_map/all_gather | solution.py:77
  78.1 0.8 slice.93
  79.0 8.7 %convert_element_type.41 = f32[16,785,256]{2,1,0:T(8,128)} convert(bf16[16,785,256]{2,1,0:T(8,128)(2,1)} %all-gather.16.cloned.1.call-done) | non-fusion elementwise | flops 3215360 | bytes 19292160 | tf_op jit(solution)/shard_map/convert_element_type | solution.py:77
  87.6 9.0 %slice_bitcast_fusion = (f32[1,196,16,256]{3,1,2,0:T(8,128)S(1)}, f32[1,196,16,256]{3,1,2,0:T(8,128)}, f32[1,196,16,256]{3,1,2,0:T(8,128)}, f32[1,196,16,256]{3,1,2,0:T(8,128)}) fusion(f32[16,785,256]{2,1,0:T(8,128)} %convert_element_type.41), kind=kLoop, calls=%fused_computation.9 | loop fusion | bytes 25690112 | tf_op jit(solution)/shard_map/stack | solution.py:97
  96.7 17.3 %pad_maximum_fusion = (f32[2,196,16,256]{3,1,2,0:T(8,128)}, f32[2,196,16,256]{3,1,2,0:T(8,128)}, f32[2,196,16,256]{3,1,2,0:T(8,128)}, f32[2,196,16,256]{3,1,2,0:T(8,128)}) fusion(f32[1,196,16,256]{3,1,2,0:T(8,128)} %get-tuple-element.29, f32[1,196,16,256]{3,1,2,0:T(8,128)} %get-tuple-element.30, f32[1,196,16,256]{3,1,2,0:T(8,128)} %get-tuple-element.28, ...), kind=kLoop, calls=%fused_computation.5 | loop fusion | flops 6422528 | bytes 38535168 | tf_op jit(solution)/shard_map/stack | solution.py:95
  114.0 39.8 %all-gather.10.cloned.1.call-done = bf16[4096,1024]{1,0:T(8,128)(2,1)} async-done(((bf16[256,1024]{1,0:T(8,128)(2,1)}), bf16[4096,1024]{1,0:T(8,128)(2,1)}) %all-gather.10.cloned.1.call-update) | async-done | bytes 8388624 | tf_op jit(solution)/shard_map/all_gather | solution.py:92
  153.8 19.0 %add_reduce_fusion = (f32[2,2]{1,0:T(2,128)S(1)}, bf16[2,2,196,16,256]{4,2,3,1,0:T(8,128)(2,1)}) fusion(f32[16,256]{1,0:T(8,128)S(1)} %bitcast.82, f32[2,196,16,256]{3,1,2,0:T(8,128)} %get-tuple-element.45, f32[2,196,16,256]{3,1,2,0:T(8,128)} %get-tuple-element.46, f32[2,196,16,256]{3,1,2,0:T(8,128)} %get-tuple-element.34, ...), kind=kOutput, calls=%fused_computation | convolution fusion | flops 6615203840 | bytes 42123280 | tf_op jit(solution)/shard_map/dot_general | solution.py:90
  172.8 6.8 %copy.44 = bf16[2,2,196,16,256]{4,3,2,1,0:T(8,128)(2,1)} copy(bf16[2,2,196,16,256]{4,2,3,1,0:T(8,128)(2,1)} %get-tuple-element.26) | data formatting | bytes 12845056 | tf_op jit(solution)/shard_map/convert_element_type | solution.py:106
  179.5 7.5 %dot_general.12 = bf16[2,2,196,4096]{3,2,1,0:T(8,128)(2,1)} reshape(bf16[2,2,196,16,256]{4,3,2,1,0:T(8,128)(2,1)} %copy.44) | data formatting | bytes 12845056 | tf_op jit(solution)/shard_map/dot_general | solution.py:107
  187.0 42.1 %all-gather.12.cloned.1.call-done = bf16[4096,1024]{1,0:T(8,128)(2,1)} async-done(((bf16[256,1024]{1,0:T(8,128)(2,1)}), bf16[4096,1024]{1,0:T(8,128)(2,1)}) %all-gather.12.cloned.1.call-update) | async-done | bytes 8388624 | tf_op jit(solution)/shard_map/all_gather | solution.py:109
  229.1 12.7 %multiply_reduce_fusion.1 = (f32[2,2]{1,0:T(2,128)S(1)}, f32[2,2,196]{2,1,0:T(2,128)S(1)}, f32[2,2,196,1024]{3,2,1,0:T(8,128)}) fusion(f32[1024]{0:T(1024)S(1)} %mul.146, f32[1024]{0:T(1024)S(1)} %mul.132, bf16[2,2,196,4096]{3,2,1,0:T(8,128)(2,1)} %dot_general.12, bf16[4096,1024]{1,0:T(8,128)(2,1)} %all-gather.12.cloned.1.call-done), kind=kOutput, calls=%fused_computation.14 | convolution fusion | flops 6579878912 | bytes 18033744 | tf_op jit(solution)/shard_map/dot_general | solution.py:107
  241.8 0.0 all-gather.14.cloned.1.call-update
  241.8 2.1 fusion.10
  243.9 1.8 copy.48
  245.7 0.0 copy-start.9
  245.7 4.0 %reshape.90 = f32[4,14,14,1024]{3,0,2,1:T(4,128)} reshape(f32[2,2,196,1024]{3,1,0,2:T(2,128)S(1)} %copy.48) | data formatting | bytes 6422528 | tf_op jit(solution)/shard_map/convert_element_type | solution.py:86
  249.7 1.1 copy.46
  250.8 0.2 reshape.88
  251.1 0.1 mul.149
  251.1 2.7 multiply_reduce_fusion
  253.9 2.0 reshape.105
  255.9 25.7 %all-gather.14.cloned.1.call-done = f32[32,196,64]{1,2,0:T(8,128)} async-done(((f32[2,196,64]{1,2,0:T(8,128)}), f32[32,196,64]{1,2,0:T(8,128)}) %all-gather.14.cloned.1.call-update) | async-done | bytes 1605648 | tf_op jit(solution)/shard_map/all_gather | solution.py:132
  281.6 3.4 %copy.49 = f32[16,2,196,64]{3,0,2,1:T(8,128)S(1)} copy(f32[16,2,196,64]{2,3,1,0:T(8,128)} %bitcast.83) | data formatting | bytes 3211264 | tf_op jit(solution)/shard_map/all_gather | solution.py:132
  285.1 1.9 fusion.11
  286.9 2.8 mul.152
  289.8 2.8 mul.155
  292.6 17.8 %multiply_reduce_fusion.3 = (f32[4]{0:T(128)S(1)}, f32[4]{0:T(128)S(1)}, f32[4,14,14,1024]{3,0,2,1:T(4,128)}) fusion(f32[14,14,1024]{2,1,0:T(8,128)} %mul.152, f32[4,14,14,1024]{3,0,2,1:T(4,128)S(1)} %copy-done, f32[14,14,1024]{2,1,0:T(8,128)} %mul.155, f32[7,7,1,1024]{3,2,1,0:T(1,128)S(1)} %reshape.88, f32[4,14,14,1024]{3,2,1,0:T(8,128)} %reshape.105), kind=kOutput, calls=%fused_computation.21 | convolution fusion | flops 368345088 | bytes 11440160 | tf_op jit(solution)/shard_map/conv_general_dilated | solution.py:120
  310.4 4.2 %reshape.89 = f32[2,2,196,1024]{3,1,0,2:T(2,128)S(1)} reshape(f32[4,14,14,1024]{3,0,2,1:T(4,128)} %get-tuple-element.44) | data formatting | bytes 6422528 | tf_op jit(solution)/shard_map/reshape | solution.py:128
  314.6 3.4 %fusion.5 = bf16[2,2,196,1024]{3,1,2,0:T(2,128)(2,1)S(1)} fusion(f32[2,2,196,1024]{3,1,0,2:T(2,128)S(1)} %reshape.89, bf16[1,2,196,1024]{3,1,2,0:T(2,128)(2,1)} %bitcast.76, bf16[1,2,196,1024]{3,1,2,0:T(2,128)(2,1)} %bitcast.79), kind=kLoop, calls=%fused_computation.19 | loop fusion | flops 3211264 | bytes 6422528 | tf_op jit(solution)/shard_map/convert.2
  318.1 2.3 slice_bitcast_fusion.4
  320.3 0.1 negate_bitcast_fusion
  320.4 0.1 reduce_sum.71
  320.5 0.7 copy.50
  (23 shorter events, 0.2 us)
Async XLA Ops:
  7.2 5.3 %copy-start.8 = (f32[49,64]{1,0:T(8,128)S(1)}, f32[49,64]{1,0:T(8,128)}, u32[]{:S(2)}) copy-start(f32[49,64]{1,0:T(8,128)} %param.26) | copy-start | bytes 37636
  7.2 5.3 %copy-start.10 = (f32[64]{0:T(128)S(1)}, f32[64]{0:T(128)}, u32[]{:S(2)}) copy-start(f32[64]{0:T(128)} %param.27) | copy-start | bytes 772
  7.2 5.3 %copy-start.11 = (f32[64]{0:T(128)S(1)}, f32[64]{0:T(128)}, u32[]{:S(2)}) copy-start(f32[64]{0:T(128)} %param.28) | copy-start | bytes 772
  7.2 5.3 %copy-start.12 = (f32[64]{0:T(128)S(1)}, f32[64]{0:T(128)}, u32[]{:S(2)}) copy-start(f32[64]{0:T(128)} %param.29) | copy-start | bytes 772
  7.2 5.3 %copy-start.13 = (f32[64]{0:T(128)S(1)}, f32[64]{0:T(128)}, u32[]{:S(2)}) copy-start(f32[64]{0:T(128)} %param.30) | copy-start | bytes 772
  7.2 5.3 %copy-start.14 = (f32[64]{0:T(128)S(1)}, f32[64]{0:T(128)}, u32[]{:S(2)}) copy-start(f32[64]{0:T(128)} %param.31) | copy-start | bytes 772
  7.2 31.9 %copy-start.6 = (f32[196,64]{0,1:T(8,128)S(1)}, f32[196,64]{0,1:T(8,128)}, u32[]{:S(2)}) copy-start(f32[196,64]{0,1:T(8,128)} %param.25) | copy-start | bytes 150532
  7.2 31.9 %copy-start.7 = (f32[196,64]{0,1:T(8,128)S(1)}, f32[196,64]{0,1:T(8,128)}, u32[]{:S(2)}) copy-start(f32[196,64]{0,1:T(8,128)} %param.24) | copy-start | bytes 150532
  7.2 32.6 %copy-start.1 = (bf16[2,196,1024]{2,0,1:T(2,128)(2,1)S(1)}, bf16[2,196,1024]{2,0,1:T(2,128)(2,1)}, u32[]{:S(2)}) copy-start(bf16[2,196,1024]{2,0,1:T(2,128)(2,1)} %param.17) | copy-start | bytes 2408452
  7.3 32.6 %copy-start.3 = (bf16[2,196,1024]{2,0,1:T(2,128)(2,1)S(1)}, bf16[2,196,1024]{2,0,1:T(2,128)(2,1)}, u32[]{:S(2)}) copy-start(bf16[2,196,1024]{2,0,1:T(2,128)(2,1)} %param.16) | copy-start | bytes 2408452
  7.3 70.8 %all-gather.16.cloned.1.call-start = ((), (), s32[]{:S(2)}) async-start(), calls=%async_computation.3 | async-start | bytes 6893568 | tf_op jit(solution)/shard_map/all_gather | solution.py:77
  10.9 142.8 %all-gather.10.cloned.1.call-start = ((), (), s32[]{:S(2)}) async-start(), calls=%async_computation | async-start | bytes 8912896 | tf_op jit(solution)/shard_map/all_gather | solution.py:92
  11.7 217.4 %all-gather.12.cloned.1.call-start = ((), (), s32[]{:S(2)}) async-start(), calls=%async_computation.1 | async-start | bytes 8912896 | tf_op jit(solution)/shard_map/all_gather | solution.py:109
  12.4 269.2 %all-gather.14.cloned.1.call-start = ((), (), s32[]{:S(2)}) async-start(), calls=%async_computation.2 | async-start | bytes 2228224 | tf_op jit(solution)/shard_map/all_gather | solution.py:132
  38.0 0.8 copy-start.5
  187.0 54.8 %copy-start.2 = (bf16[2,196,1024]{2,0,1:T(2,128)(2,1)S(1)}, bf16[2,196,1024]{2,0,1:T(2,128)(2,1)}, u32[]{:S(2)}) copy-start(bf16[2,196,1024]{2,0,1:T(2,128)(2,1)} %param.17) | copy-start | bytes 2408452
  187.0 54.8 %copy-start.4 = (bf16[2,196,1024]{2,0,1:T(2,128)(2,1)S(1)}, bf16[2,196,1024]{2,0,1:T(2,128)(2,1)}, u32[]{:S(2)}) copy-start(bf16[2,196,1024]{2,0,1:T(2,128)(2,1)} %param.16) | copy-start | bytes 2408452
  245.7 5.4 %copy-start.9 = (f32[196]{0:T(256)S(1)}, f32[196]{0:T(256)}, u32[]{:S(2)}) copy-start(f32[196]{0:T(256)} %param.23) | copy-start | bytes 2356
  286.9 5.6 %copy-start = (f32[4,14,14,1024]{3,0,2,1:T(4,128)S(1)}, f32[4,14,14,1024]{3,0,2,1:T(4,128)}, u32[]{:S(2)}) copy-start(f32[4,14,14,1024]{3,0,2,1:T(4,128)} %reshape.90) | copy-start | bytes 9633796
Sparse Core Ops, SparseCore 0:
  11.0 67.0 all-gather.15
  80.2 73.4 all-gather.9
  155.9 73.1 all-gather.11
  241.9 39.6 all-gather.13

commit v3 on v2

--- a/solution.py
+++ b/solution.py
@@ -128,9 +128,12 @@
     ).reshape(2, nrows, npix, chans)
     total = coef + conv
     box = jnp.stack([box_center, box_radius])
+    if (npix * cl) % 128 == 0:
+        box = box.reshape(2, npix * cl // 128, 128)
     box, _ = lax.optimization_barrier((box, normed))
-    box_g = lax.all_gather(box, "spec", axis=0, tiled=False)
+    box_g = lax.all_gather(box, "spec", axis=0, tiled=False).reshape(nsh, 2, npix, cl)
     box_full = box_g.transpose(1, 2, 0, 3).reshape(2, npix, nsh * cl)
+    total, box_full = lax.optimization_barrier((total, box_full))
     center, radius = box_full[0], box_full[1]
     linear = jnp.sum(total * center, axis=(2, 3))
     spread = jnp.sum(jnp.abs(total) * radius, axis=(2, 3))

time: 328 us -> 311 us (0.948)
  waiting for transfers between devices: 143 us -> 125 us
  other arithmetic: 40.3 us -> 47.8 us
  local copies, waits for them, and re-layouts: 55.5 us -> 50.5 us
    all_gather x1, waiting for transfers between devices: 25.7 us -> 8.12 us  [local(): lax.all_gather(box, 'spec', axis=0, tiled=False).reshape(nsh, 2, npix, cl)]
    reduce_sum x0 -> x1, other arithmetic: none -> 7.3 us  [local(): linear = jnp.sum(total * center, axis=(2, 3))]
    add x0 -> x1, other arithmetic: none -> 5.83 us  [local(): total = coef + conv]
    convert_element_type x2 -> x0, local copies, waits for them, and re-layouts: 5.8 us -> none  [local(): coef = jnp.stack([lower_coef, upper_coef]).astype(jnp.float32)]
    all_gather x1 -> x0, local copies, waits for them, and re-layouts: 3.42 us -> none  [local(): box_g = lax.all_gather(box, 'spec', axis=0, tiled=False)]
    another operation x1 -> x0, other arithmetic: 3.42 us -> none
  transfers between devices with their start and end apart: 4 -> 4, of which waited for: 4 -> 4; matrix products, arithmetic and copies ran while one was open for 27% -> 34% of each run, Pallas kernels for 0% -> 0%
where the time goes in v3:
time: 311 us; the launch traced here: 310 us
  waiting for transfers between devices  125 us (40%)
  local copies, waits for them, and re-layouts  50.5 us (16%)
  other arithmetic  47.8 us (15%)
  matrix products  47.3 us (15%)
  blocking collectives  25.4 us (8%)
  between operations  14 us (5%)
    all_gather x1, waiting for transfers between devices, local(): lax.all_gather(w_up, 'spec', axis=0, tiled=True)  42.1 us
    all_gather x1, waiting for transfers between devices, local(): lax.all_gather(w_down, 'spec', axis=0, tiled=True)  39.8 us
    all_gather x1, waiting for transfers between devices, local(): lax.all_gather(relax, 'spec', axis=0, tiled=False).astype(jnp.float32)  33.4 us
    all_gather x1, blocking collectives, local(): small_g = lax.all_gather(small, 'spec', axis=0, tiled=False)  25.4 us
    dot_general x1, matrix products, local(): jnp.dot(flat, lax.all_gather(w_down, 'spec', axis=0, tiled=True).T, prefe...  19 us
    another operation x1, other arithmetic, local(): first = jnp.stack([s0, s1])[:, None]  17.2 us
    conv_general_dilated x1, matrix products, local(): lax.conv_general_dilated(centered.reshape(2 * nrows, MAP, MAP, chans), ta...  15.7 us
    dot_general x1, matrix products, local(): jnp.dot(relaxed16, lax.all_gather(w_up, 'spec', axis=0, tiled=True), pref...  12.7 us
  transfers between devices with their start and end apart: 4, of which 4 were waited for; matrix products, arithmetic and copies ran while one was open for 34% of the time, Pallas kernels for 0%

profile of v3, /device:TPU:0, one launch (start us, length us, event | category | flops | bytes accessed | tf_op | source)
XLA Modules:
  0.0 310.1 jit_solution(4939508023672842738)
XLA Ops:
  7.2 0.0 copy-start.7
  7.2 0.0 copy-start.9
  7.2 0.0 copy-start.10
  7.2 0.0 copy-start.11
  7.2 0.0 copy-start.12
  7.2 0.0 copy-start.13
  7.2 0.0 copy-start.5
  7.2 0.0 copy-start.6
  7.2 0.0 copy-start.1
  7.3 0.0 copy-start.2
  7.3 0.0 all-gather.16.cloned.1.call-start
  7.3 0.8 broadcast_in_dim.29
  8.1 0.9 copy.41
  9.1 1.0 copy.40
  10.1 0.8 maximum_bitcast_fusion
  10.9 0.0 all-gather.16.cloned.1.call-update
  10.9 0.0 all-gather.10.cloned.1.call-start
  11.0 0.7 all-gather.10.cloned.1.call-update
  11.7 0.0 all-gather.12.cloned.1.call-start
  11.7 0.7 all-gather.12.cloned.1.call-update
  12.4 0.0 all-gather.14.cloned.1.call-start
  12.5 25.4 %all-gather.3 = f32[16,54,64]{2,1,0:T(8,128)S(1)} all-gather(f32[1,54,64]{2,1,0:T(8,128)S(1)} %bitcast.78), channel_id=2, replica_groups=mesh['grp'=2,'spec'=16] {'spec'}, dimensions={0}, use_global_device_ids=true | all-gather | bytes 235008 | tf_op jit(solution)/shard_map/all_gather | solution.py:64
  38.0 0.8 copy-done.3
  38.7 0.1 slice_reduce_fusion.2
  38.9 0.1 mul.144
  38.9 0.1 mul.130
  39.0 0.1 mul.134
  39.1 0.1 mul.123
  39.2 0.1 copy.47
  39.3 0.1 stack.58
  39.4 0.1 copy.46
  39.4 0.1 stack.57
  39.5 0.6 pad_maximum_fusion.5
  40.2 4.5 %fusion.5 = (f32[2,2]{1,0:T(2,128)S(1)}, bf16[2,2,196,1024,1]{3,1,2,0,4:T(2,128)(2,1)}) fusion(f32[1024]{0:T(1024)S(1)} %mul.134, f32[1024]{0:T(1024)S(1)} %mul.123, bf16[1,2,196,1024]{3,1,2,0:T(2,128)(2,1)S(1)} %bitcast.70, bf16[1,2,196,1024]{3,1,2,0:T(2,128)(2,1)S(1)} %bitcast.72), kind=kLoop, calls=%fused_computation.20 | loop fusion | flops 4816892 | bytes 3219472 | tf_op jit(solution)/shard_map/reduce_sum | solution.py:88
  44.7 33.4 %all-gather.16.cloned.1.call-done = bf16[16,785,256]{2,1,0:T(8,128)(2,1)} async-done(((bf16[1,785,256]{2,1,0:T(8,128)(2,1)}), bf16[16,785,256]{2,1,0:T(8,128)(2,1)}) %all-gather.16.cloned.1.call-update) | async-done | bytes 6430736 | tf_op jit(solution)/shard_map/all_gather | solution.py:77
  78.1 0.8 slice.86
  79.0 8.7 %convert_element_type.31 = f32[16,785,256]{2,1,0:T(8,128)} convert(bf16[16,785,256]{2,1,0:T(8,128)(2,1)} %all-gather.16.cloned.1.call-done) | non-fusion elementwise | flops 3215360 | bytes 19292160 | tf_op jit(solution)/shard_map/convert_element_type | solution.py:77
  87.6 9.1 %slice_bitcast_fusion = (f32[1,196,16,256]{3,1,2,0:T(8,128)S(1)}, f32[1,196,16,256]{3,1,2,0:T(8,128)}, f32[1,196,16,256]{3,1,2,0:T(8,128)}, f32[1,196,16,256]{3,1,2,0:T(8,128)}) fusion(f32[16,785,256]{2,1,0:T(8,128)} %convert_element_type.31), kind=kLoop, calls=%fused_computation.11 | loop fusion | bytes 25690112 | tf_op jit(solution)/shard_map/stack | solution.py:97
  96.7 17.2 %pad_maximum_fusion = (f32[2,196,16,256]{3,1,2,0:T(8,128)}, f32[2,196,16,256]{3,1,2,0:T(8,128)}, f32[2,196,16,256]{3,1,2,0:T(8,128)}, f32[2,196,16,256]{3,1,2,0:T(8,128)}) fusion(f32[1,196,16,256]{3,1,2,0:T(8,128)} %get-tuple-element.27, f32[1,196,16,256]{3,1,2,0:T(8,128)} %get-tuple-element.28, f32[1,196,16,256]{3,1,2,0:T(8,128)} %get-tuple-element.26, ...), kind=kLoop, calls=%fused_computation.5 | loop fusion | flops 6422528 | bytes 38535168 | tf_op jit(solution)/shard_map/stack | solution.py:95
  113.9 39.8 %all-gather.10.cloned.1.call-done = bf16[4096,1024]{1,0:T(8,128)(2,1)} async-done(((bf16[256,1024]{1,0:T(8,128)(2,1)}), bf16[4096,1024]{1,0:T(8,128)(2,1)}) %all-gather.10.cloned.1.call-update) | async-done | bytes 8388624 | tf_op jit(solution)/shard_map/all_gather | solution.py:92
  153.8 19.0 %add_reduce_fusion = (f32[2,2]{1,0:T(2,128)S(1)}, bf16[2,2,196,16,256]{4,2,3,1,0:T(8,128)(2,1)}) fusion(f32[16,256]{1,0:T(8,128)S(1)} %bitcast.73, f32[2,196,16,256]{3,1,2,0:T(8,128)} %get-tuple-element.43, f32[2,196,16,256]{3,1,2,0:T(8,128)} %get-tuple-element.44, f32[2,196,16,256]{3,1,2,0:T(8,128)} %get-tuple-element.32, ...), kind=kOutput, calls=%fused_computation | convolution fusion | flops 6615203840 | bytes 42123280 | tf_op jit(solution)/shard_map/dot_general | solution.py:90
  172.7 6.8 %copy.42 = bf16[2,2,196,16,256]{4,3,2,1,0:T(8,128)(2,1)} copy(bf16[2,2,196,16,256]{4,2,3,1,0:T(8,128)(2,1)} %get-tuple-element.24) | data formatting | bytes 12845056 | tf_op jit(solution)/shard_map/convert_element_type | solution.py:106
  179.5 7.5 %dot_general.12 = bf16[2,2,196,4096]{3,2,1,0:T(8,128)(2,1)} reshape(bf16[2,2,196,16,256]{4,3,2,1,0:T(8,128)(2,1)} %copy.42) | data formatting | bytes 12845056 | tf_op jit(solution)/shard_map/dot_general | solution.py:107
  187.0 42.1 %all-gather.12.cloned.1.call-done = bf16[4096,1024]{1,0:T(8,128)(2,1)} async-done(((bf16[256,1024]{1,0:T(8,128)(2,1)}), bf16[4096,1024]{1,0:T(8,128)(2,1)}) %all-gather.12.cloned.1.call-update) | async-done | bytes 8388624 | tf_op jit(solution)/shard_map/all_gather | solution.py:109
  229.1 12.7 %multiply_reduce_fusion.1 = (f32[2,2]{1,0:T(2,128)S(1)}, f32[2,2,196]{2,1,0:T(2,128)S(1)}, f32[2,2,196,1024]{3,2,1,0:T(8,128)}) fusion(f32[1024]{0:T(1024)S(1)} %mul.144, f32[1024]{0:T(1024)S(1)} %mul.130, bf16[2,2,196,4096]{3,2,1,0:T(8,128)(2,1)} %dot_general.12, bf16[4096,1024]{1,0:T(8,128)(2,1)} %all-gather.12.cloned.1.call-done), kind=kOutput, calls=%fused_computation.16 | convolution fusion | flops 6579878912 | bytes 18033744 | tf_op jit(solution)/shard_map/dot_general | solution.py:107
  241.8 0.0 all-gather.14.cloned.1.call-update
  241.8 0.1 copy.44
  241.9 0.2 reshape.81
  242.2 0.1 mul.147
  242.2 0.0 copy-done.8
  242.2 2.8 multiply_reduce_fusion
  245.0 2.0 reshape.100
  247.0 15.7 %fusion.6 = f32[4,14,14,1024]{3,0,2,1:T(4,128)S(1)} fusion(f32[7,7,1,1024]{3,2,1,0:T(1,128)S(1)} %reshape.81, f32[4,14,14,1024]{3,2,1,0:T(8,128)} %reshape.100), kind=kOutput, calls=%fused_computation.21 | convolution fusion | flops 363528192 | bytes 6623232 | tf_op jit(solution)/shard_map/conv_general_dilated | solution.py:120
  262.7 3.7 %reshape.82 = f32[2,2,196,1024]{3,1,0,2:T(2,128)} reshape(f32[4,14,14,1024]{3,0,2,1:T(4,128)S(1)} %fusion.6) | data formatting | bytes 6422528 | tf_op jit(solution)/shard_map/reshape | solution.py:128
  266.4 5.8 %convert_add_fusion = f32[2,2,196,1024]{3,1,2,0:T(2,128)} fusion(f32[2,2,196,1024]{3,1,0,2:T(2,128)} %reshape.82, bf16[1,2,196,1024]{3,1,2,0:T(2,128)(2,1)} %bitcast.69, bf16[1,2,196,1024]{3,1,2,0:T(2,128)(2,1)} %bitcast.71), kind=kLoop, calls=%fused_computation.9 | loop fusion | flops 2408448 | bytes 8028160 | tf_op jit(solution)/shard_map/add | solution.py:129
  272.2 8.1 %all-gather.14.cloned.1.call-done = f32[32,98,128]{2,1,0:T(8,128)} async-done(((f32[2,98,128]{2,1,0:T(8,128)}), f32[32,98,128]{2,1,0:T(8,128)}) %all-gather.14.cloned.1.call-update) | async-done | bytes 1605648 | tf_op jit(solution)/shard_map/all_gather | solution.py:134
  280.3 2.5 reshape.83
  282.9 2.4 copy.48
  285.3 3.2 %slice_bitcast_fusion.4 = (f32[196,1024]{0,1:T(8,128)}, f32[196,1024]{0,1:T(8,128)}) fusion(f32[2,196,1024]{1,2,0:T(8,128)} %bitcast.68), kind=kLoop, calls=%fused_computation.30 | loop fusion | bytes 3211264 | tf_op jit(solution)/shard_map/mul | solution.py:139
  288.4 2.5 copy.49
  290.9 2.5 copy.50
  293.3 7.3 %multiply_reduce_fusion.3 = (f32[2,2]{1,0:T(2,128)S(1)}, f32[2,2]{1,0:T(2,128)S(1)}, bf16[2,2,196,1024]{3,1,2,0:T(2,128)(2,1)S(1)}) fusion(f32[2,2,196,1024]{3,1,2,0:T(2,128)S(1)} %copy-done, f32[196,1024]{1,0:T(8,128)} %copy.49, f32[196,1024]{1,0:T(8,128)} %copy.50), kind=kLoop, calls=%fused_computation.24 | loop fusion | flops 4816888 | bytes 6422560 | tf_op jit(solution)/shard_map/reduce_sum | solution.py:138
  300.6 2.3 slice_bitcast_fusion.6
  302.9 0.7 copy.51
  (23 shorter events, 0.2 us)
Async XLA Ops:
  7.2 5.3 %copy-start.7 = (f32[49,64]{1,0:T(8,128)S(1)}, f32[49,64]{1,0:T(8,128)}, u32[]{:S(2)}) copy-start(f32[49,64]{1,0:T(8,128)} %param.26) | copy-start | bytes 37636
  7.2 5.3 %copy-start.9 = (f32[64]{0:T(128)S(1)}, f32[64]{0:T(128)}, u32[]{:S(2)}) copy-start(f32[64]{0:T(128)} %param.27) | copy-start | bytes 772
  7.2 5.3 %copy-start.10 = (f32[64]{0:T(128)S(1)}, f32[64]{0:T(128)}, u32[]{:S(2)}) copy-start(f32[64]{0:T(128)} %param.28) | copy-start | bytes 772
  7.2 5.3 %copy-start.11 = (f32[64]{0:T(128)S(1)}, f32[64]{0:T(128)}, u32[]{:S(2)}) copy-start(f32[64]{0:T(128)} %param.29) | copy-start | bytes 772
  7.2 5.3 %copy-start.12 = (f32[64]{0:T(128)S(1)}, f32[64]{0:T(128)}, u32[]{:S(2)}) copy-start(f32[64]{0:T(128)} %param.30) | copy-start | bytes 772
  7.2 5.3 %copy-start.13 = (f32[64]{0:T(128)S(1)}, f32[64]{0:T(128)}, u32[]{:S(2)}) copy-start(f32[64]{0:T(128)} %param.31) | copy-start | bytes 772
  7.2 31.9 %copy-start.5 = (f32[196,64]{0,1:T(8,128)S(1)}, f32[196,64]{0,1:T(8,128)}, u32[]{:S(2)}) copy-start(f32[196,64]{0,1:T(8,128)} %param.25) | copy-start | bytes 150532
  7.2 32.1 %copy-start.6 = (f32[196,64]{0,1:T(8,128)S(1)}, f32[196,64]{0,1:T(8,128)}, u32[]{:S(2)}) copy-start(f32[196,64]{0,1:T(8,128)} %param.24) | copy-start | bytes 150532
  7.2 32.9 %copy-start.1 = (bf16[2,196,1024]{2,0,1:T(2,128)(2,1)S(1)}, bf16[2,196,1024]{2,0,1:T(2,128)(2,1)}, u32[]{:S(2)}) copy-start(bf16[2,196,1024]{2,0,1:T(2,128)(2,1)} %param.17) | copy-start | bytes 2408452
  7.3 32.9 %copy-start.2 = (bf16[2,196,1024]{2,0,1:T(2,128)(2,1)S(1)}, bf16[2,196,1024]{2,0,1:T(2,128)(2,1)}, u32[]{:S(2)}) copy-start(bf16[2,196,1024]{2,0,1:T(2,128)(2,1)} %param.16) | copy-start | bytes 2408452
  7.3 70.8 %all-gather.16.cloned.1.call-start = ((), (), s32[]{:S(2)}) async-start(), calls=%async_computation.3 | async-start | bytes 6893568 | tf_op jit(solution)/shard_map/all_gather | solution.py:77
  10.9 142.8 %all-gather.10.cloned.1.call-start = ((), (), s32[]{:S(2)}) async-start(), calls=%async_computation | async-start | bytes 8912896 | tf_op jit(solution)/shard_map/all_gather | solution.py:92
  11.7 217.4 %all-gather.12.cloned.1.call-start = ((), (), s32[]{:S(2)}) async-start(), calls=%async_computation.1 | async-start | bytes 8912896 | tf_op jit(solution)/shard_map/all_gather | solution.py:109
  12.4 267.9 %all-gather.14.cloned.1.call-start = ((), (), s32[]{:S(2)}) async-start(), calls=%async_computation.2 | async-start | bytes 1810432 | tf_op jit(solution)/shard_map/all_gather | solution.py:134
  38.0 0.8 copy-start.3
  187.0 54.8 %copy-start.4 = (f32[16,54,64]{2,1,0:T(8,128)S(1)}, f32[16,54,64]{2,1,0:T(8,128)}, u32[]{:S(2)}) copy-start(f32[16,54,64]{2,1,0:T(8,128)} %copy-done.3) | copy-start | bytes 663556
  187.0 55.2 %copy-start.8 = (f32[196]{0:T(256)S(1)}, f32[196]{0:T(256)}, u32[]{:S(2)}) copy-start(f32[196]{0:T(256)} %param.23) | copy-start | bytes 2356
  285.3 8.1 %copy-start = (f32[2,2,196,1024]{3,1,2,0:T(2,128)S(1)}, f32[2,2,196,1024]{3,1,2,0:T(2,128)}, u32[]{:S(2)}) copy-start(f32[2,2,196,1024]{3,1,2,0:T(2,128)} %convert_add_fusion) | copy-start | bytes 9633796
Sparse Core Ops, SparseCore 0:
  11.0 67.0 all-gather.15
  80.2 73.4 all-gather.9
  155.9 73.1 all-gather.11
  241.9 38.3 all-gather.13

commit v4 on v3

--- a/solution.py
+++ b/solution.py
@@ -66,51 +66,75 @@
     kernel_taps = small_full[:ntap]
     conv_bias, gain, norm_bias, gamma, out_bias = (small_full[ntap + i] for i in range(5))
 
-    relax = jnp.concatenate(
-        [
-            slopes.transpose(1, 2, 0).reshape(2 * npix, hl),
-            intercepts.transpose(1, 2, 0).reshape(2 * npix, hl),
-            pw1_bias[None],
-        ],
-        axis=0,
-    )
+    gi = lax.axis_index("grp")
+    half = hl // 2
+
+    def halves(a):
+        own = lax.dynamic_slice_in_dim(a, gi * half, half, 0)
+        other = lax.dynamic_slice_in_dim(a, (1 - gi) * half, half, 0)
+        return own, other
+
+    swap = [(0, 1), (1, 0)]
+    down_own = lax.all_gather(halves(w_down)[0], "spec", axis=0, tiled=True)
+    up_own = lax.all_gather(halves(w_up)[0], "spec", axis=0, tiled=True)
+    down_other = lax.ppermute(down_own, "grp", swap)
+    up_other = lax.ppermute(up_own, "grp", swap)
+
+    def relax_pack(sl, ic, hb):
+        return jnp.concatenate(
+            [
+                sl.transpose(1, 2, 0).reshape(2 * npix, half),
+                ic.transpose(1, 2, 0).reshape(2 * npix, half),
+                hb[None],
+            ],
+            axis=0,
+        )
+
+    sl_h, ic_h, hb_h = halves(slopes), halves(intercepts), halves(pw1_bias)
+    relax = jnp.stack([relax_pack(sl_h[i], ic_h[i], hb_h[i]) for i in range(2)])
     relax_g = lax.all_gather(relax, "spec", axis=0, tiled=False).astype(jnp.float32)
-
-    def relax_map(i):
-        return relax_g[:, i * npix : (i + 1) * npix].transpose(1, 0, 2)
-
-    s0, s1, c0, c1 = (relax_map(i) for i in range(4))
-    hid_bias = relax_g[:, 4 * npix]
 
     height = 2 * nrows * npix
     coef = jnp.stack([lower_coef, upper_coef]).astype(jnp.float32)
     scaled = coef * gamma
     bias = jnp.sum(scaled * out_bias, axis=(2, 3))
     flat = scaled.astype(jnp.bfloat16).reshape(height, chans)
-    hidden = jnp.dot(
-        flat,
-        lax.all_gather(w_down, "spec", axis=0, tiled=True).T,
-        preferred_element_type=jnp.float32,
-    ).reshape(2, nrows, npix, nsh, hl)
-    first = jnp.stack([s0, s1])[:, None]
-    second = jnp.stack([s1, s0])[:, None]
-    first_icpt = jnp.stack([c0, c1])[:, None]
-    second_icpt = jnp.stack([c1, c0])[:, None]
-    positive = jnp.maximum(hidden, 0.0)
-    negative = jnp.minimum(hidden, 0.0)
-    relaxed = positive * first + negative * second
-    extra = jnp.sum(
-        positive * first_icpt + negative * second_icpt + relaxed * hid_bias,
-        axis=(2, 3, 4),
-    )
-    relaxed16 = relaxed.astype(jnp.bfloat16).reshape(height, -1)
-    normed = jnp.dot(
-        relaxed16,
-        lax.all_gather(w_up, "spec", axis=0, tiled=True),
-        preferred_element_type=jnp.float32,
-    )
+
+    def relax_half(h, w_dn, w_u):
+        rg = relax_g[:, h]
+
+        def relax_map(i):
+            return rg[:, i * npix : (i + 1) * npix].transpose(1, 0, 2)
+
+        s0, s1, c0, c1 = (relax_map(i) for i in range(4))
+        hid_bias = rg[:, 4 * npix]
+        hidden = jnp.dot(flat, w_dn.T, preferred_element_type=jnp.float32).reshape(
+            2, nrows, npix, nsh, half
+        )
+        first = jnp.stack([s0, s1])[:, None]
+        second = jnp.stack([s1, s0])[:, None]
+        first_icpt = jnp.stack([c0, c1])[:, None]
+        second_icpt = jnp.stack([c1, c0])[:, None]
+        positive = jnp.maximum(hidden, 0.0)
+        negative = jnp.minimum(hidden, 0.0)
+        relaxed = positive * first + negative * second
+        part = jnp.sum(
+            positive * first_icpt + negative * second_icpt + relaxed * hid_bias,
+            axis=(2, 3, 4),
+        )
+        relaxed16 = relaxed.astype(jnp.bfloat16).reshape(height, -1)
+        return jnp.dot(relaxed16, w_u, preferred_element_type=jnp.float32), part
+
+    normed_a, extra_a = relax_half(0, down_own, up_own)
+    normed_b, extra_b = relax_half(1, down_other, up_other)
+    normed = normed_a + normed_b
+    extra = extra_a + extra_b
     bias = bias + extra
     normed = normed.reshape(2, nrows, npix, chans)
+    box = jnp.stack([box_center, box_radius])
+    if (npix * cl) % 128 == 0:
+        box = box.reshape(2, npix * cl // 128, 128)
+    box, normed = lax.optimization_barrier((box, normed))
     bias = bias + jnp.sum(normed * norm_bias, axis=(2, 3))
     tilted = normed * gain
     centered = ln_scale[None, None, :, None] * (tilted - jnp.mean(tilted, axis=-1, keepdims=True))
@@ -127,10 +151,6 @@
         precision=lax.Precision.HIGHEST,
     ).reshape(2, nrows, npix, chans)
     total = coef + conv
-    box = jnp.stack([box_center, box_radius])
-    if (npix * cl) % 128 == 0:
-        box = box.reshape(2, npix * cl // 128, 128)
-    box, _ = lax.optimization_barrier((box, normed))
     box_g = lax.all_gather(box, "spec", axis=0, tiled=False).reshape(nsh, 2, npix, cl)
     box_full = box_g.transpose(1, 2, 0, 3).reshape(2, npix, nsh * cl)
     total, box_full = lax.optimization_barrier((total, box_full))

time: 311 us -> 339 us (1.090)
  waiting for transfers between devices: 125 us -> 156 us
  other arithmetic: 47.8 us -> 34.4 us
  local copies, waits for them, and re-layouts: 50.5 us -> 58.1 us
    all_gather x1, waiting for transfers between devices: 33.4 us -> 62.8 us  [local(): lax.all_gather(relax, 'spec', axis=0, tiled=False).astype(jnp.float32)]
    ppermute x0 -> x2, waiting for transfers between devices: none -> 19.9 us  [the longest x1 19.9 us: local(): down_other = lax.ppermute(down_own, 'grp', swap)]
    another operation x1 -> x7, other arithmetic: 17.2 us -> 2.52 us  [the longest x2 0.85 us: relax_half(): first_icpt = jnp.stack([c0, c1])[:, None]]
    all_gather x2, waiting for transfers between devices: 81.9 us -> 70.4 us  [the longest x1 49.8 us: local(): down_own = lax.all_gather(halves(w_down)[0], 'spec', axis=0, tiled=True)]
    squeeze x0 -> x1, local copies, waits for them, and re-layouts: none -> 10.2 us  [relax_half(): rg = relax_g[:, h]]
    dot_general x1 -> x0, local copies, waits for them, and re-layouts: 7.48 us -> none  [local(): jnp.dot(relaxed16, lax.all_gather(w_up, 'spec', axis=0, tiled=True), pref...]
    all_gather x1, waiting for transfers between devices: 8.12 us -> 2.57 us  [local(): lax.all_gather(box, 'spec', axis=0, tiled=False).reshape(nsh, 2, npix, cl)]
    another operation x1 -> x2, local copies, waits for them, and re-layouts: 9.05 us -> 6.77 us  [relax_half(): first_icpt = jnp.stack([c0, c1])[:, None]]
  transfers between devices with their start and end apart: 4 -> 6, of which waited for: 4 -> 5; matrix products, arithmetic and copies ran while one was open for 34% -> 31% of each run, Pallas kernels for 0% -> 0%
where the time goes in v4:
time: 339 us; the launch traced here: 338 us
  waiting for transfers between devices  156 us (46%)
  local copies, waits for them, and re-layouts  58.1 us (17%)
  matrix products  47.5 us (14%)
  other arithmetic  34.4 us (10%)
  blocking collectives  25.4 us (7%)
  between operations  14.2 us (4%)
    all_gather x1, waiting for transfers between devices, local(): lax.all_gather(relax, 'spec', axis=0, tiled=False).astype(jnp.float32)  62.8 us
    all_gather x1, waiting for transfers between devices, local(): down_own = lax.all_gather(halves(w_down)[0], 'spec', axis=0, tiled=True)  49.8 us
    all_gather x1, blocking collectives, local(): small_g = lax.all_gather(small, 'spec', axis=0, tiled=False)  25.4 us
    all_gather x1, waiting for transfers between devices, local(): up_own = lax.all_gather(halves(w_up)[0], 'spec', axis=0, tiled=True)  20.6 us
    ppermute x1, waiting for transfers between devices, local(): down_other = lax.ppermute(down_own, 'grp', swap)  19.9 us
    dot_general x2, matrix products, relax_half(): jnp.dot(flat, w_dn.T, preferred_element_type=jnp.float32)  18.9 us
    conv_general_dilated x1, matrix products, local(): lax.conv_general_dilated(centered.reshape(2 * nrows, MAP, MAP, chans), ta...  16 us
    dot_general x2, matrix products, relax_half(): return (jnp.dot(relaxed16, w_u, preferred_element_type=jnp.float32), part)  12.6 us
  transfers between devices with their start and end apart: 6, of which 5 were waited for; matrix products, arithmetic and copies ran while one was open for 31% of the time, Pallas kernels for 0%

profile of v4, /device:TPU:0, one launch (start us, length us, event | category | flops | bytes accessed | tf_op | source)
XLA Modules:
  0.0 338.3 jit_solution(3138993793243098966)
XLA Ops:
  7.3 0.9 copy-done
  8.2 0.7 constant_dynamic-slice_fusion
  9.0 0.0 all-gather.9.cloned.1.call-start
  9.1 1.8 constant_dynamic-slice_fusion.1
  10.9 0.0 all-gather.13.cloned.1.call-start
  11.0 1.3 dynamic-slice_bitcast_fusion.2
  12.5 0.1 dynamic-slice_bitcast_fusion.5
  12.6 0.8 pad_maximum_fusion.9
  13.5 0.1 copy.65
  13.6 0.1 stack.91
  13.7 0.1 copy.64
  13.8 0.1 stack.90
  14.0 25.4 %all-gather.3 = f32[16,54,64]{2,1,0:T(8,128)S(1)} all-gather(f32[1,54,64]{2,1,0:T(8,128)S(1)} %bitcast.124), channel_id=2, replica_groups=mesh['grp'=2,'spec'=16] {'spec'}, dimensions={0}, use_global_device_ids=true | all-gather | bytes 235008 | tf_op jit(solution)/shard_map/all_gather | solution.py:64
  39.3 0.1 slice_reduce_fusion.2
  39.5 0.1 mul.195
  39.5 0.1 mul.178
  39.6 0.6 pad_maximum_fusion.10
  40.3 4.5 %fusion.4 = (f32[2,2]{1,0:T(2,128)S(1)}, bf16[2,2,196,1024,1]{3,1,2,0,4:T(2,128)(2,1)}) fusion(f32[1024]{0:T(1024)S(1)} %mul.195, f32[1024]{0:T(1024)S(1)} %mul.178, bf16[1,2,196,1024]{3,1,2,0:T(2,128)(2,1)S(1)} %bitcast.116, bf16[1,2,196,1024]{3,1,2,0:T(2,128)(2,1)S(1)} %bitcast.118), kind=kLoop, calls=%fused_computation.23 | loop fusion | flops 4816892 | bytes 3219472 | tf_op jit(solution)/shard_map/reduce_sum | solution.py:100
  44.8 20.6 %all-gather.11.cloned.1.call-done = bf16[2048,1024]{1,0:T(8,128)(2,1)} async-done(((bf16[128,1024]{1,0:T(8,128)(2,1)}), bf16[2048,1024]{1,0:T(8,128)(2,1)}) %all-gather.11.cloned.1.call-update) | async-done | bytes 4194320 | tf_op jit(solution)/shard_map/all_gather | solution.py:79
  65.4 1.5 collective-permute-start.1
  66.8 49.8 %all-gather.9.cloned.1.call-done = bf16[2048,1024]{1,0:T(8,128)(2,1)} async-done(((bf16[128,1024]{1,0:T(8,128)(2,1)}), bf16[2048,1024]{1,0:T(8,128)(2,1)}) %all-gather.9.cloned.1.call-update) | async-done | bytes 4194320 | tf_op jit(solution)/shard_map/all_gather | solution.py:78
  116.6 1.5 collective-permute-start
  118.1 62.8 %all-gather.13.cloned.1.call-done = bf16[32,785,128]{2,1,0:T(8,128)(2,1)} async-done(((bf16[2,785,128]{2,1,0:T(8,128)(2,1)}), bf16[32,785,128]{2,1,0:T(8,128)(2,1)}) %all-gather.13.cloned.1.call-update) | async-done | bytes 6430736 | tf_op jit(solution)/shard_map/all_gather | solution.py:95
  180.9 8.3 %convert.5 = f32[16,2,785,128]{3,2,1,0:T(8,128)} convert(bf16[16,2,785,128]{3,2,1,0:T(8,128)(2,1)} %bitcast.113) | non-fusion elementwise | flops 3215360 | bytes 19292160 | tf_op jit(solution)/shard_map/convert_element_type | solution.py:95
  189.2 10.2 %slice_bitcast_fusion = (f32[16,785,128]{2,1,0:T(8,128)}, f32[16,785,128]{2,1,0:T(8,128)}) fusion(f32[16,2,785,128]{3,2,1,0:T(8,128)} %convert.5), kind=kLoop, calls=%fused_computation.6 | loop fusion | bytes 25722880 | tf_op jit(solution)/shard_map/squeeze | solution.py:104
  199.4 0.8 slice.118
  200.3 3.4 slice_bitcast_fusion.4
  203.7 0.4 pad_maximum_fusion.4
  204.1 0.4 pad_maximum_fusion
  204.5 9.4 %add_reduce_fusion.1 = (f32[2,2]{1,0:T(2,128)S(1)}, bf16[2,2,196,16,128]{4,2,3,1,0:T(8,128)(2,1)}) fusion(f32[16,128]{1,0:T(8,128)S(1)} %bitcast.123, f32[2,196,16,128]{3,1,2,0:T(8,128)S(1)} %get-tuple-element.42, f32[2,196,16,128]{3,1,2,0:T(8,128)S(1)} %get-tuple-element.41, f32[2,196,16,128]{3,1,2,0:T(8,128)S(1)} %get-tuple-element.46, ...), kind=kOutput, calls=%fused_computation.1 | convolution fusion | flops 3307601920 | bytes 21864464 | tf_op jit(solution)/shard_map/dot_general | solution.py:111
  214.0 2.4 copy.71
  216.4 0.8 slice.121
  217.2 3.4 slice_bitcast_fusion.2
  220.6 0.4 pad_maximum_fusion.6
  221.0 0.4 pad_maximum_fusion.2
  221.5 1.7 copy-done.16
  223.2 5.2 %fusion.8 = f32[784,1024]{1,0:T(8,128)} fusion(bf16[2048,1024]{1,0:T(8,128)(2,1)S(1)} %copy-done.16, bf16[98,8,16,128]{3,2,1,0:T(8,128)(2,1)S(1)} %bitcast.114), kind=kOutput, calls=%fused_computation.27 | convolution fusion | flops 3288334336 | bytes 10616832 | tf_op jit(solution)/shard_map/dot_general | solution.py:126
  228.4 19.9 %collective-permute-done = bf16[2048,1024]{1,0:T(8,128)(2,1)} collective-permute-done((bf16[2048,1024]{1,0:T(8,128)(2,1)}, bf16[2048,1024]{1,0:T(8,128)(2,1)}, u32[]{:S(2)}, u32[]{:S(2)}) %collective-permute-start) | collective-permute-done | bytes 4194336 | tf_op jit(solution)/shard_map/ppermute | solution.py:80
  248.3 9.4 %add_reduce_fusion = (f32[2,2]{1,0:T(2,128)S(1)}, bf16[2,2,196,16,128]{4,2,3,1,0:T(8,128)(2,1)}) fusion(f32[16,128]{1,0:T(8,128)S(1)} %bitcast.122, f32[2,196,16,128]{3,1,2,0:T(8,128)S(1)} %get-tuple-element.40, f32[2,196,16,128]{3,1,2,0:T(8,128)S(1)} %get-tuple-element.39, f32[2,196,16,128]{3,1,2,0:T(8,128)S(1)} %get-tuple-element.44, ...), kind=kOutput, calls=%fused_computation | convolution fusion | flops 3307601920 | bytes 21864464 | tf_op jit(solution)/shard_map/dot_general | solution.py:111
  257.7 2.5 copy.73
  260.3 0.3 copy-done.17
  260.6 7.4 %fusion.13 = f32[784,1024]{1,0:T(8,128)} fusion(f32[784,1024]{1,0:T(8,128)S(1)} %copy-done.17, bf16[2048,1024]{1,0:T(8,128)(2,1)} %collective-permute-done.1, bf16[98,8,16,128]{3,2,1,0:T(8,128)(2,1)S(1)} %bitcast.115), kind=kOutput, calls=%fused_computation.35 | convolution fusion | flops 3289137152 | bytes 13828096 | tf_op jit(solution)/shard_map/dot_general | solution.py:126
  268.0 3.3 reshape.108
  271.3 0.1 copy.75
  271.4 0.2 reshape.110
  271.7 0.1 mul.215
  271.7 0.1 mul.212
  271.8 0.1 mul.191
  271.9 2.7 multiply_reduce_fusion.1
  274.6 0.2 copy-done.2
  274.8 2.4 multiply_reduce_fusion
  277.2 3.4 %reshape.126 = f32[4,14,14,1024]{3,2,1,0:T(8,128)} reshape(f32[2,2,196,1024]{3,2,1,0:T(8,128)} %get-tuple-element.24) | data formatting | bytes 6422528 | tf_op jit(solution)/shard_map/reshape | solution.py:145
  280.6 16.0 %fusion.11 = f32[4,14,14,1024]{3,0,2,1:T(4,128)} fusion(f32[7,7,1,1024]{3,2,1,0:T(1,128)S(1)} %reshape.110, f32[4,14,14,1024]{3,2,1,0:T(8,128)} %reshape.126), kind=kOutput, calls=%fused_computation.30 | convolution fusion | flops 363528192 | bytes 6623232 | tf_op jit(solution)/shard_map/conv_general_dilated | solution.py:144
  296.7 5.5 %reshape.111 = f32[2,2,196,1024]{3,1,0,2:T(2,128)} reshape(f32[4,14,14,1024]{3,0,2,1:T(4,128)} %fusion.11) | data formatting | bytes 6422528 | tf_op jit(solution)/shard_map/reshape | solution.py:152
  302.2 5.3 %convert_add_fusion = f32[2,2,196,1024]{3,1,2,0:T(2,128)} fusion(f32[2,2,196,1024]{3,1,0,2:T(2,128)} %reshape.111, bf16[1,2,196,1024]{3,1,2,0:T(2,128)(2,1)S(1)} %bitcast.117, bf16[1,2,196,1024]{3,1,2,0:T(2,128)(2,1)S(1)} %bitcast.119), kind=kLoop, calls=%fused_computation.8 | loop fusion | flops 2408448 | bytes 8028160 | tf_op jit(solution)/shard_map/add | solution.py:153
  307.5 2.6 all-gather.15.cloned.1.call-done
  310.0 3.6 %reshape.112 = f32[16,2,196,64]{3,2,1,0:T(8,128)} reshape(f32[32,98,128]{2,1,0:T(8,128)} %all-gather.15.cloned.1.call-done) | data formatting | bytes 3211264 | tf_op jit(solution)/shard_map/reshape | solution.py:154
  313.6 2.6 copy.77
  316.2 1.5 slice_bitcast_fusion.10
  317.7 1.5 copy.78
  319.3 1.6 copy.79
  320.9 8.0 %multiply_reduce_fusion.3 = (f32[2,2]{1,0:T(2,128)S(1)}, f32[2,2]{1,0:T(2,128)S(1)}, bf16[2,2,196,1024]{3,1,2,0:T(2,128)(2,1)S(1)}) fusion(f32[2,2,196,1024]{3,1,2,0:T(2,128)} %convert_add_fusion, f32[196,1024]{1,0:T(8,128)S(1)} %copy.78, f32[196,1024]{1,0:T(8,128)S(1)} %copy.79), kind=kLoop, calls=%fused_computation.33 | loop fusion | flops 4816888 | bytes 6422560 | tf_op jit(solution)/shard_map/reduce_sum | solution.py:158
  328.9 2.3 slice_bitcast_fusion.12
  331.1 0.7 copy.80
  (53 shorter events, 0.5 us)
Async XLA Ops:
  7.2 1.1 copy-start
  7.2 5.3 %copy-start.9 = (bf16[256]{0:T(256)(128)(2,1)S(1)}, bf16[256]{0:T(256)(128)(2,1)}, u32[]{:S(2)}) copy-start(bf16[256]{0:T(256)(128)(2,1)} %param.20) | copy-start | bytes 1540
  7.2 6.3 %copy-start.6 = (f32[196,64]{0,1:T(8,128)S(1)}, f32[196,64]{0,1:T(8,128)}, u32[]{:S(2)}) copy-start(f32[196,64]{0,1:T(8,128)} %param.25) | copy-start | bytes 150532
  7.2 6.5 %copy-start.7 = (f32[196,64]{0,1:T(8,128)S(1)}, f32[196,64]{0,1:T(8,128)}, u32[]{:S(2)}) copy-start(f32[196,64]{0,1:T(8,128)} %param.24) | copy-start | bytes 150532
  7.2 58.2 %all-gather.11.cloned.1.call-start = ((), (), s32[]{:S(2)}) async-start(), calls=%async_computation.1 | async-start | bytes 4456448 | tf_op jit(solution)/shard_map/all_gather | solution.py:79
  8.2 5.7 %copy-start.8 = (f32[49,64]{1,0:T(8,128)S(1)}, f32[49,64]{1,0:T(8,128)}, u32[]{:S(2)}) copy-start(f32[49,64]{1,0:T(8,128)} %param.26) | copy-start | bytes 37636
  8.2 5.7 %copy-start.11 = (f32[64]{0:T(128)S(1)}, f32[64]{0:T(128)}, u32[]{:S(2)}) copy-start(f32[64]{0:T(128)} %param.27) | copy-start | bytes 772
  8.2 5.7 %copy-start.12 = (f32[64]{0:T(128)S(1)}, f32[64]{0:T(128)}, u32[]{:S(2)}) copy-start(f32[64]{0:T(128)} %param.28) | copy-start | bytes 772
  8.2 5.7 %copy-start.13 = (f32[64]{0:T(128)S(1)}, f32[64]{0:T(128)}, u32[]{:S(2)}) copy-start(f32[64]{0:T(128)} %param.29) | copy-start | bytes 772
  8.2 5.7 %copy-start.14 = (f32[64]{0:T(128)S(1)}, f32[64]{0:T(128)}, u32[]{:S(2)}) copy-start(f32[64]{0:T(128)} %param.30) | copy-start | bytes 772
  8.2 5.7 %copy-start.15 = (f32[64]{0:T(128)S(1)}, f32[64]{0:T(128)}, u32[]{:S(2)}) copy-start(f32[64]{0:T(128)} %param.31) | copy-start | bytes 772
  9.0 31.2 %copy-start.3 = (bf16[2,196,1024]{2,0,1:T(2,128)(2,1)S(1)}, bf16[2,196,1024]{2,0,1:T(2,128)(2,1)}, u32[]{:S(2)}) copy-start(bf16[2,196,1024]{2,0,1:T(2,128)(2,1)} %param.17) | copy-start | bytes 2408452
  9.0 31.2 %copy-start.4 = (bf16[2,196,1024]{2,0,1:T(2,128)(2,1)S(1)}, bf16[2,196,1024]{2,0,1:T(2,128)(2,1)}, u32[]{:S(2)}) copy-start(bf16[2,196,1024]{2,0,1:T(2,128)(2,1)} %param.16) | copy-start | bytes 2408452
  9.0 107.6 %all-gather.9.cloned.1.call-start = ((), (), s32[]{:S(2)}) async-start(), calls=%async_computation | async-start | bytes 4456448 | tf_op jit(solution)/shard_map/all_gather | solution.py:78
  10.9 170.0 %all-gather.13.cloned.1.call-start = ((), (), s32[]{:S(2)}) async-start(), calls=%async_computation.2 | async-start | bytes 6893568 | tf_op jit(solution)/shard_map/all_gather | solution.py:95
  13.5 296.6 %all-gather.15.cloned.1.call-start = ((), (), s32[]{:S(2)}) async-start(), calls=%async_computation.3 | async-start | bytes 1810432 | tf_op jit(solution)/shard_map/all_gather | solution.py:154
  65.4 194.9 %collective-permute-start.1 = (bf16[2048,1024]{1,0:T(8,128)(2,1)}, bf16[2048,1024]{1,0:T(8,128)(2,1)}, u32[]{:S(2)}, u32[]{:S(2)}) collective-permute-start(bf16[2048,1024]{1,0:T(8,128)(2,1)} %all-gather.11.cloned.1.call-done), channel_id=1, source_target_pairs={{0,16},{16,0},{1,17},{17,1},{2,18},{18,2},{3,19},{19,3},{4,20},{20... | collective-permute-start | bytes 12582920 | tf_op jit(solution)/shard_map/ppermute | solution.py:81
  116.6 131.7 %collective-permute-start = (bf16[2048,1024]{1,0:T(8,128)(2,1)}, bf16[2048,1024]{1,0:T(8,128)(2,1)}, u32[]{:S(2)}, u32[]{:S(2)}) collective-permute-start(bf16[2048,1024]{1,0:T(8,128)(2,1)} %all-gather.9.cloned.1.call-done), channel_id=1, source_target_pairs={{0,16},{16,0},{1,17},{17,1},{2,18},{18,2},{3,19},{19,3},{4,20},{20... | collective-permute-start | bytes 12582920 | tf_op jit(solution)/shard_map/ppermute | solution.py:80
  221.0 2.2 copy-start.16
  257.7 2.9 copy-start.17
  271.3 3.3 copy-start.10
  271.9 2.9 copy-start.2
  296.7 5.6 %copy-start.5 = (bf16[2,196,1024]{2,0,1:T(2,128)(2,1)S(1)}, bf16[2,196,1024]{2,0,1:T(2,128)(2,1)}, u32[]{:S(2)}) copy-start(bf16[2,196,1024]{2,0,1:T(2,128)(2,1)} %param.16) | copy-start | bytes 2408452
  319.3 12.5 %copy-start.1 = (bf16[256,1024]{1,0:T(8,128)(2,1)S(1)}, bf16[256,1024]{1,0:T(8,128)(2,1)}, u32[]{:S(2)}) copy-start(bf16[256,1024]{1,0:T(8,128)(2,1)} %param.19) | copy-start | bytes 1572868
Sparse Core Ops, SparseCore 0:
  10.8 54.5 all-gather.10
  67.5 49.0 all-gather.8
  119.4 61.5 all-gather.12
  271.4 38.5 all-gather.14

commit v5 on v2

--- a/solution.py
+++ b/solution.py
@@ -74,7 +74,40 @@
         ],
         axis=0,
     )
-    relax_g = lax.all_gather(relax, "spec", axis=0, tiled=False).astype(jnp.float32)
+    nrelax = relax.shape[0]
+
+    def rows_of(flat):
+        pad = (-flat.shape[0]) % chans
+        return jnp.pad(flat, (0, pad)).reshape(-1, chans)
+
+    pack1 = jnp.concatenate([w_down, rows_of(relax.reshape(-1))], axis=0)
+    gath1 = lax.all_gather(pack1, "spec", axis=0, tiled=False)
+    wd_full = gath1[:, :hl].reshape(nsh * hl, chans)
+    relax_g = (
+        gath1[:, hl:]
+        .reshape(nsh, -1)[:, : nrelax * hl]
+        .reshape(nsh, nrelax, hl)
+        .astype(jnp.float32)
+    )
+
+    box = jnp.stack([box_center, box_radius])
+    box_hi = lax.reduce_precision(box, exponent_bits=8, mantissa_bits=7)
+    box_rest = box - box_hi
+    box_mid = lax.reduce_precision(box_rest, exponent_bits=8, mantissa_bits=7)
+    box_lo = box_rest - box_mid
+    box_parts = jnp.stack([box_hi, box_mid, box_lo]).astype(jnp.bfloat16)
+    nbox = box_parts.size
+    pack2 = jnp.concatenate([w_up, rows_of(box_parts.reshape(-1))], axis=0)
+    pack2, gath1 = lax.optimization_barrier((pack2, gath1))
+    gath2 = lax.all_gather(pack2, "spec", axis=0, tiled=False)
+    wu_full = gath2[:, :hl].reshape(nsh * hl, chans)
+    box_g = (
+        gath2[:, hl:]
+        .reshape(nsh, -1)[:, :nbox]
+        .reshape(nsh, 3, 2, npix, cl)
+        .astype(jnp.float32)
+    )
+    box_g = (box_g[:, 0] + box_g[:, 1]) + box_g[:, 2]
 
     def relax_map(i):
         return relax_g[:, i * npix : (i + 1) * npix].transpose(1, 0, 2)
@@ -89,7 +122,7 @@
     flat = scaled.astype(jnp.bfloat16).reshape(height, chans)
     hidden = jnp.dot(
         flat,
-        lax.all_gather(w_down, "spec", axis=0, tiled=True).T,
+        wd_full.T,
         preferred_element_type=jnp.float32,
     ).reshape(2, nrows, npix, nsh, hl)
     first = jnp.stack([s0, s1])[:, None]
@@ -106,7 +139,7 @@
     relaxed16 = relaxed.astype(jnp.bfloat16).reshape(height, -1)
     normed = jnp.dot(
         relaxed16,
-        lax.all_gather(w_up, "spec", axis=0, tiled=True),
+        wu_full,
         preferred_element_type=jnp.float32,
     )
     bias = bias + extra
@@ -127,10 +160,8 @@
         precision=lax.Precision.HIGHEST,
     ).reshape(2, nrows, npix, chans)
     total = coef + conv
-    box = jnp.stack([box_center, box_radius])
-    box, _ = lax.optimization_barrier((box, normed))
-    box_g = lax.all_gather(box, "spec", axis=0, tiled=False)
     box_full = box_g.transpose(1, 2, 0, 3).reshape(2, npix, nsh * cl)
+    total, box_full = lax.optimization_barrier((total, box_full))
     center, radius = box_full[0], box_full[1]
     linear = jnp.sum(total * center, axis=(2, 3))
     spread = jnp.sum(jnp.abs(total) * radius, axis=(2, 3))

time: 328 us -> 327 us (level)
  waiting for transfers between devices: 143 us -> 108 us
  local copies, waits for them, and re-layouts: 55.5 us -> 71.1 us
  other arithmetic: 40.3 us -> 54.3 us
    all_gather x4 -> x2, waiting for transfers between devices: 141 us -> 108 us  [the longest x1 86.4 us: local(): gath1 = lax.all_gather(pack1, 'spec', axis=0, tiled=False)]
    convert_element_type x3, local copies, waits for them, and re-layouts: 12.6 us -> 24.4 us  [the longest x1 12.9 us: local(): relax_g = gath1[:, hl:].reshape(nsh, -1)[:, :nrelax * hl].reshape(nsh, nr...]
    reduce_sum x0 -> x1, other arithmetic: none -> 8.06 us  [local(): linear = jnp.sum(total * center, axis=(2, 3))]
    dot_general x1 -> x0, local copies, waits for them, and re-layouts: 7.52 us -> none  [local(): jnp.dot(relaxed16, lax.all_gather(w_up, 'spec', axis=0, tiled=True), pref...]
    unnamed x32 -> x34, local copies, waits for them, and re-layouts: 1.48 us -> 8.35 us
    another operation x1, other arithmetic: 17.3 us -> 11.3 us  [local(): first = jnp.stack([s0, s1])[:, None]]
    add x0 -> x1, other arithmetic: none -> 5.81 us  [local(): total = coef + conv]
    dot_general x2, matrix products: 31.7 us -> 36.9 us  [the longest x1 21.2 us: local(): jnp.dot(flat, wd_full.T, preferred_element_type=jnp.float32)]
  transfers between devices with their start and end apart: 4 -> 2, of which waited for: 4 -> 2; matrix products, arithmetic and copies ran while one was open for 27% -> 23% of each run, Pallas kernels for 0% -> 0%
where the time goes in v5:
time: 327 us; the launch traced here: 326 us
  waiting for transfers between devices  108 us (33%)
  local copies, waits for them, and re-layouts  71.1 us (22%)
  other arithmetic  54.3 us (17%)
  matrix products  52.6 us (16%)
  blocking collectives  25.9 us (8%)
  between operations  14.3 us (4%)
    all_gather x1, waiting for transfers between devices, local(): gath1 = lax.all_gather(pack1, 'spec', axis=0, tiled=False)  86.4 us
    all_gather x1, blocking collectives, local(): small_g = lax.all_gather(small, 'spec', axis=0, tiled=False)  25.9 us
    all_gather x1, waiting for transfers between devices, local(): gath2 = lax.all_gather(pack2, 'spec', axis=0, tiled=False)  21.3 us
    dot_general x1, matrix products, local(): jnp.dot(flat, wd_full.T, preferred_element_type=jnp.float32)  21.2 us
    dot_general x1, matrix products, local(): normed = jnp.dot(relaxed16, wu_full, preferred_element_type=jnp.float32)  15.8 us
    conv_general_dilated x1, matrix products, local(): lax.conv_general_dilated(centered.reshape(2 * nrows, MAP, MAP, chans), ta...  15.6 us
    convert_element_type x1, local copies, waits for them, and re-layouts, local(): relax_g = gath1[:, hl:].reshape(nsh, -1)[:, :nrelax * hl].reshape(nsh, nr...  12.9 us
    convert_element_type x1, local copies, waits for them, and re-layouts, local(): box_g = gath2[:, hl:].reshape(nsh, -1)[:, :nbox].reshape(nsh, 3, 2, npix,...  11.3 us
  transfers between devices with their start and end apart: 2, of which 2 were waited for; matrix products, arithmetic and copies ran while one was open for 23% of the time, Pallas kernels for 0%

profile of v5, /device:TPU:0, one launch (start us, length us, event | category | flops | bytes accessed | tf_op | source)
XLA Modules:
  0.0 326.1 jit_solution(924987058178801036)
XLA Ops:
  7.2 0.0 all-gather.9.cloned.1.call-start
  7.2 1.0 copy.35
  8.3 1.0 copy.36
  9.2 0.0 copy-start.8
  9.2 0.0 copy-start.10
  9.3 0.0 copy-start.11
  9.3 0.0 copy-start.12
  9.3 0.0 copy-start.13
  9.3 0.0 copy-start.14
  9.4 0.7 broadcast_in_dim.29
  10.1 0.1 reshape.209
  10.2 0.2 reshape.210
  10.5 0.0 copy-start.5
  10.5 1.0 maximum_bitcast_fusion
  11.5 0.0 all-gather.9.cloned.1.call-update
  11.5 0.0 all-gather.11.cloned.1.call-start
  11.5 0.0 copy-done.8
  11.6 0.0 copy-done.10
  11.6 0.0 copy-done.11
  11.6 0.0 copy-done.12
  11.6 25.9 %all-gather.3 = f32[16,54,64]{2,1,0:T(8,128)S(1)} all-gather(f32[1,54,64]{2,1,0:T(8,128)S(1)} %bitcast.100), channel_id=2, replica_groups=mesh['grp'=2,'spec'=16] {'spec'}, dimensions={0}, use_global_device_ids=true | all-gather | bytes 235008 | tf_op jit(solution)/shard_map/all_gather | solution.py:64
  37.5 0.1 slice_reduce_fusion.2
  37.7 0.1 mul.123
  37.7 0.1 mul.134
  37.9 0.2 copy.38
  38.1 0.2 convert_element_type.47
  38.3 0.1 reshape.212
  38.4 0.1 mul.130
  38.5 0.1 mul.144
  38.5 0.1 mul.147
  38.6 0.1 copy.40
  38.7 0.2 reshape.214
  39.0 0.9 pad_maximum_fusion.5
  39.9 4.5 %fusion.11 = (f32[2,2]{1,0:T(2,128)S(1)}, bf16[2,2,196,1024,1]{3,1,2,0,4:T(2,128)(2,1)}) fusion(f32[1024]{0:T(1024)S(1)} %mul.134, f32[1024]{0:T(1024)S(1)} %mul.123, bf16[1,2,196,1024]{3,1,2,0:T(2,128)(2,1)S(1)} %bitcast.91, bf16[1,2,196,1024]{3,1,2,0:T(2,128)(2,1)S(1)} %bitcast.93), kind=kLoop, calls=%fused_computation.31 | loop fusion | flops 4816892 | bytes 3219472 | tf_op jit(solution)/shard_map/reduce_sum | solution.py:121
  44.4 86.4 %all-gather.9.cloned.1.call-done = bf16[16,453,1024]{2,1,0:T(8,128)(2,1)} async-done(((bf16[1,453,1024]{2,1,0:T(8,128)(2,1)}), bf16[16,453,1024]{2,1,0:T(8,128)(2,1)}) %all-gather.9.cloned.1.call-update) | async-done | bytes 14843920 | tf_op jit(solution)/shard_map/all_gather | solution.py:84
  130.8 2.9 slice-done
  133.7 6.3 %copy.54 = bf16[2,8,197,1024]{3,1,2,0:T(8,128)(2,1)} copy(bf16[2,8,197,1024]{3,2,1,0:T(8,128)(2,1)S(1)} %bitcast.85) | data formatting | bytes 12910592
  140.0 0.0 all-gather.11.cloned.1.call-update
  140.0 7.6 %slice_convert_fusion = f32[16,200960]{1,0:T(8,128)} fusion(bf16[16,201728]{1,0:T(8,128)(2,1)} %bitcast.86), kind=kLoop, calls=%fused_computation.14 | loop fusion | flops 3215360 | bytes 19292160 | tf_op jit(solution)/shard_map/convert_element_type | solution.py:90
  147.6 12.9 %reshape.218 = f32[16,785,256]{2,1,0:T(8,128)} reshape(f32[16,200960]{1,0:T(8,128)} %slice_convert_fusion) | data formatting | bytes 25722880 | tf_op jit(solution)/shard_map/convert_element_type | solution.py:90
  160.5 0.9 slice.131
  161.4 8.9 %slice_bitcast_fusion.4 = (f32[1,196,16,256]{3,1,2,0:T(8,128)S(1)}, f32[1,196,16,256]{3,1,2,0:T(8,128)}, f32[1,196,16,256]{3,1,2,0:T(8,128)}, f32[1,196,16,256]{3,1,2,0:T(8,128)}) fusion(f32[16,785,256]{2,1,0:T(8,128)} %reshape.218), kind=kLoop, calls=%fused_computation.17 | loop fusion | bytes 25690112 | tf_op jit(solution)/shard_map/stack | solution.py:130
  170.3 11.3 %pad_maximum_fusion = (f32[2,196,16,256]{3,1,2,0:T(8,128)}, f32[2,196,16,256]{3,1,2,0:T(8,128)}) fusion(f32[1,196,16,256]{3,1,2,0:T(8,128)} %get-tuple-element.25, f32[1,196,16,256]{3,1,2,0:T(8,128)} %get-tuple-element.26), kind=kLoop, calls=%fused_computation.7 | loop fusion | flops 3211264 | bytes 19267584 | tf_op jit(solution)/shard_map/stack | solution.py:128
  181.6 5.4 %pad_maximum_fusion.2 = (f32[2,196,16,256]{3,1,2,0:T(8,128)}, f32[2,196,16,256]{3,1,2,0:T(8,128)}) fusion(f32[1,196,16,256]{3,1,2,0:T(8,128)S(1)} %get-tuple-element.23, f32[1,196,16,256]{3,1,2,0:T(8,128)S(1)} %copy-done), kind=kLoop, calls=%fused_computation.9 | loop fusion | flops 3211264 | bytes 19267584 | tf_op jit(solution)/shard_map/stack | solution.py:130
  187.0 21.2 %add_reduce_fusion = (f32[2,2]{1,0:T(2,128)S(1)}, f32[2,2,196,16,256]{4,2,3,1,0:T(8,128)}) fusion(f32[16,256]{1,0:T(8,128)S(1)} %bitcast.94, f32[2,196,16,256]{3,1,2,0:T(8,128)} %get-tuple-element.28, f32[2,196,16,256]{3,1,2,0:T(8,128)} %get-tuple-element.27, f32[2,196,16,256]{3,1,2,0:T(8,128)} %get-tuple-element.30, ...), kind=kOutput, calls=%fused_computation | convolution fusion | flops 6611992576 | bytes 49070096 | tf_op jit(solution)/shard_map/dot_general | solution.py:123
  208.1 21.3 %all-gather.11.cloned.1.call-done = bf16[16,330,1024]{2,1,0:T(8,128)(2,1)} async-done(((bf16[1,330,1024]{2,1,0:T(8,128)(2,1)}), bf16[16,330,1024]{2,1,0:T(8,128)(2,1)}) %all-gather.11.cloned.1.call-update) | async-done | bytes 10813456 | tf_op jit(solution)/shard_map/all_gather | solution.py:102
  229.4 15.8 %fusion.8 = (f32[2,2]{1,0:T(2,128)S(1)}, f32[2,2,196]{2,1,0:T(2,128)S(1)}, f32[2,2,196,1024,1]{3,2,4,1,0:T(8,128)}) fusion(f32[1024]{0:T(1024)S(1)} %mul.144, f32[1024]{0:T(1024)S(1)} %mul.130, bf16[16,330,1024]{2,1,0:T(8,128)(2,1)} %all-gather.11.cloned.1.call-done, f32[2,2,196,16,256]{4,2,3,1,0:T(8,128)} %get-tuple-element.45, ...), kind=kOutput, calls=%fused_computation.26 | convolution fusion | flops 6599146496 | bytes 37825616 | tf_op jit(solution)/shard_map/dot_general | solution.py:140
  245.2 2.8 multiply_reduce_fusion
  248.0 2.1 reshape.236
  250.1 15.6 %fusion.12 = f32[4,14,14,1024]{3,0,2,1:T(4,128)S(1)} fusion(f32[7,7,1,1024]{3,2,1,0:T(1,128)S(1)} %reshape.214, f32[4,14,14,1024]{3,2,1,0:T(8,128)} %reshape.236), kind=kOutput, calls=%fused_computation.32 | convolution fusion | flops 363528192 | bytes 6623232 | tf_op jit(solution)/shard_map/conv_general_dilated | solution.py:153
  265.7 3.7 %reshape.215 = f32[2,2,196,1024]{3,1,0,2:T(2,128)} reshape(f32[4,14,14,1024]{3,0,2,1:T(4,128)S(1)} %fusion.12) | data formatting | bytes 6422528 | tf_op jit(solution)/shard_map/reshape | solution.py:161
  269.4 5.8 %convert_add_fusion = f32[2,2,196,1024]{3,1,2,0:T(2,128)} fusion(f32[2,2,196,1024]{3,1,0,2:T(2,128)} %reshape.215, bf16[1,2,196,1024]{3,1,2,0:T(2,128)(2,1)} %bitcast.90, bf16[1,2,196,1024]{3,1,2,0:T(2,128)(2,1)} %bitcast.92), kind=kLoop, calls=%fused_computation.15 | loop fusion | flops 2408448 | bytes 8028160 | tf_op jit(solution)/shard_map/add | solution.py:162
  275.2 1.7 slice-done.1
  276.9 1.3 copy.55
  278.3 2.5 slice_convert_fusion.1
  280.7 11.3 %reshape.219 = f32[16,3,2,196,64]{4,3,2,1,0:T(8,128)} reshape(f32[16,75264]{1,0:T(8,128)} %slice_convert_fusion.1) | data formatting | bytes 9633792 | tf_op jit(solution)/shard_map/convert_element_type | solution.py:108
  292.1 4.4 %fusion.7 = f32[2,196,16,64]{3,1,0,2:T(8,128)S(1)} fusion(f32[16,3,2,196,64]{4,3,2,1,0:T(8,128)} %reshape.219), kind=kLoop, calls=%fused_computation.20 | loop fusion | flops 802816 | bytes 6422528 | tf_op jit(solution)/shard_map/transpose | solution.py:163
  296.5 2.4 copy.42
  298.9 3.2 slice_bitcast_fusion.8
  302.0 2.4 copy.43
  304.5 2.4 copy.44
  306.9 8.1 %multiply_reduce_fusion.2 = (f32[2,2]{1,0:T(2,128)S(1)}, f32[2,2]{1,0:T(2,128)S(1)}, bf16[2,2,196,1024]{3,1,2,0:T(2,128)(2,1)}) fusion(f32[2,2,196,1024]{3,1,2,0:T(2,128)S(1)} %copy-done.1, f32[196,1024]{1,0:T(8,128)} %copy.43, f32[196,1024]{1,0:T(8,128)} %copy.44), kind=kLoop, calls=%fused_computation.35 | loop fusion | flops 4816888 | bytes 6422560 | tf_op jit(solution)/shard_map/reduce_sum | solution.py:166
  315.0 0.7 copy.45
  315.6 3.6 %slice_bitcast_fusion.10 = (bf16[2,196,1024]{2,0,1:T(2,128)(2,1)}, bf16[2,196,1024]{2,0,1:T(2,128)(2,1)}) fusion(bf16[2,2,196,1024]{3,1,2,0:T(2,128)(2,1)} %get-tuple-element.31), kind=kLoop, calls=%fused_computation.44 | loop fusion | bytes 3211264 | tf_op jit(solution)/shard_map/convert_element_type | solution.py:169
  (33 shorter events, 0.3 us)
Async XLA Ops:
  7.2 3.3 %copy-start.4 = (bf16[256,1024]{1,0:T(8,128)(2,1)S(1)}, bf16[256,1024]{1,0:T(8,128)(2,1)}, u32[]{:S(2)}) copy-start(bf16[256,1024]{1,0:T(8,128)(2,1)} %param.18) | copy-start | bytes 1572868
  7.2 123.6 %all-gather.9.cloned.1.call-start = ((), (), s32[]{:S(2)}) async-start(), calls=%async_computation | async-start | bytes 15876096 | tf_op jit(solution)/shard_map/all_gather | solution.py:84
  9.2 2.3 copy-start.8
  9.2 2.3 copy-start.10
  9.3 2.3 copy-start.11
  9.3 2.3 copy-start.12
  9.3 2.3 copy-start.13
  9.3 2.3 copy-start.14
  10.0 27.8 %copy-start.6 = (f32[196,64]{0,1:T(8,128)S(1)}, f32[196,64]{0,1:T(8,128)}, u32[]{:S(2)}) copy-start(f32[196,64]{0,1:T(8,128)} %param.25) | copy-start | bytes 150532
  10.0 27.8 %copy-start.7 = (f32[196,64]{0,1:T(8,128)S(1)}, f32[196,64]{0,1:T(8,128)}, u32[]{:S(2)}) copy-start(f32[196,64]{0,1:T(8,128)} %param.24) | copy-start | bytes 150532
  10.5 28.5 %copy-start.5 = (bf16[256,1024]{1,0:T(8,128)(2,1)S(1)}, bf16[256,1024]{1,0:T(8,128)(2,1)}, u32[]{:S(2)}) copy-start(bf16[256,1024]{1,0:T(8,128)(2,1)} %param.19) | copy-start | bytes 1572868
  11.5 28.4 %copy-start.2 = (bf16[2,196,1024]{2,0,1:T(2,128)(2,1)S(1)}, bf16[2,196,1024]{2,0,1:T(2,128)(2,1)}, u32[]{:S(2)}) copy-start(bf16[2,196,1024]{2,0,1:T(2,128)(2,1)} %param.17) | copy-start | bytes 2408452
  11.5 28.4 %copy-start.3 = (bf16[2,196,1024]{2,0,1:T(2,128)(2,1)S(1)}, bf16[2,196,1024]{2,0,1:T(2,128)(2,1)}, u32[]{:S(2)}) copy-start(bf16[2,196,1024]{2,0,1:T(2,128)(2,1)} %param.16) | copy-start | bytes 2408452
  11.5 217.9 %all-gather.11.cloned.1.call-start = ((), (), s32[]{:S(2)}) async-start(), calls=%async_computation.1 | async-start | bytes 11698176 | tf_op jit(solution)/shard_map/all_gather | solution.py:102
  130.8 2.9 slice-start
  170.3 11.3 %copy-start = (f32[1,196,16,256]{3,1,2,0:T(8,128)S(1)}, f32[1,196,16,256]{3,1,2,0:T(8,128)}, u32[]{:S(2)}) copy-start(f32[1,196,16,256]{3,1,2,0:T(8,128)} %get-tuple-element.24) | copy-start | bytes 9633796
  229.4 15.8 %copy-start.9 = (f32[196]{0:T(256)S(1)}, f32[196]{0:T(256)}, u32[]{:S(2)}) copy-start(f32[196]{0:T(256)} %param.23) | copy-start | bytes 2356
  275.2 1.7 slice-start.1
  298.9 8.1 %copy-start.1 = (f32[2,2,196,1024]{3,1,2,0:T(2,128)S(1)}, f32[2,2,196,1024]{3,1,2,0:T(2,128)}, u32[]{:S(2)}) copy-start(f32[2,2,196,1024]{3,1,2,0:T(2,128)} %convert_add_fusion) | copy-start | bytes 9633796
Sparse Core Ops, SparseCore 0:
  11.6 119.1 all-gather.8
  140.1 89.2 all-gather.10

commit v6 on v2

--- a/solution.py
+++ b/solution.py
@@ -68,49 +68,80 @@
 
     relax = jnp.concatenate(
         [
-            slopes.transpose(1, 2, 0).reshape(2 * npix, hl),
-            intercepts.transpose(1, 2, 0).reshape(2 * npix, hl),
-            pw1_bias[None],
+            slopes.reshape(hl, 2 * npix),
+            intercepts.reshape(hl, 2 * npix),
+            pw1_bias[:, None],
         ],
-        axis=0,
+        axis=1,
     )
-    relax_g = lax.all_gather(relax, "spec", axis=0, tiled=False).astype(jnp.float32)
+    nrel = relax.shape[1]
 
-    def relax_map(i):
-        return relax_g[:, i * npix : (i + 1) * npix].transpose(1, 0, 2)
+    box = jnp.stack([box_center, box_radius])
+    box_hi = lax.reduce_precision(box, exponent_bits=8, mantissa_bits=7)
+    box_rest = box - box_hi
+    box_mid = lax.reduce_precision(box_rest, exponent_bits=8, mantissa_bits=7)
+    box_lo = box_rest - box_mid
+    box_flat = jnp.stack([box_hi, box_mid, box_lo]).astype(jnp.bfloat16).reshape(-1)
+    nbox = box_flat.shape[0]
+    box_cols = jnp.pad(box_flat, (0, (-nbox) % hl)).reshape(hl, -1)
+    nbc = box_cols.shape[1]
 
-    s0, s1, c0, c1 = (relax_map(i) for i in range(4))
-    hid_bias = relax_g[:, 4 * npix]
+    pack1 = jnp.concatenate([w_down, relax, box_cols], axis=1)
+    gath1 = lax.all_gather(pack1, "spec", axis=0, tiled=True)
+    wd_full = gath1[:, :chans]
+    rel_g = gath1[:, chans : chans + nrel].astype(jnp.float32)
+    box_g = (
+        gath1[:, chans + nrel :]
+        .reshape(nsh, hl * nbc)[:, :nbox]
+        .reshape(nsh, 3, 2, npix, cl)
+        .astype(jnp.float32)
+    )
+    box_g = (box_g[:, 0] + box_g[:, 1]) + box_g[:, 2]
+    up_in, gath1 = lax.optimization_barrier((w_up, gath1))
+    wu_full = lax.all_gather(up_in, "spec", axis=0, tiled=True)
 
-    height = 2 * nrows * npix
+    sl = rel_g[:, : 2 * npix].reshape(-1, 2, npix)
+    ic = rel_g[:, 2 * npix : 4 * npix].reshape(-1, 2, npix)
+    hid_bias = rel_g[:, 4 * npix][:, None]
+
     coef = jnp.stack([lower_coef, upper_coef]).astype(jnp.float32)
     scaled = coef * gamma
     bias = jnp.sum(scaled * out_bias, axis=(2, 3))
-    flat = scaled.astype(jnp.bfloat16).reshape(height, chans)
-    hidden = jnp.dot(
-        flat,
-        lax.all_gather(w_down, "spec", axis=0, tiled=True).T,
-        preferred_element_type=jnp.float32,
-    ).reshape(2, nrows, npix, nsh, hl)
-    first = jnp.stack([s0, s1])[:, None]
-    second = jnp.stack([s1, s0])[:, None]
-    first_icpt = jnp.stack([c0, c1])[:, None]
-    second_icpt = jnp.stack([c1, c0])[:, None]
-    positive = jnp.maximum(hidden, 0.0)
-    negative = jnp.minimum(hidden, 0.0)
-    relaxed = positive * first + negative * second
-    extra = jnp.sum(
-        positive * first_icpt + negative * second_icpt + relaxed * hid_bias,
-        axis=(2, 3, 4),
-    )
-    relaxed16 = relaxed.astype(jnp.bfloat16).reshape(height, -1)
-    normed = jnp.dot(
-        relaxed16,
-        lax.all_gather(w_up, "spec", axis=0, tiled=True),
-        preferred_element_type=jnp.float32,
-    )
+    scaled16 = scaled.astype(jnp.bfloat16)
+
+    normed_rows = []
+    extra_rows = []
+    for s in range(2):
+        first, second = sl[:, s], sl[:, 1 - s]
+        first_icpt, second_icpt = ic[:, s], ic[:, 1 - s]
+        for r in range(nrows):
+            hidden_t = lax.dot_general(
+                wd_full,
+                scaled16[s, r],
+                (((1,), (1,)), ((), ())),
+                preferred_element_type=jnp.float32,
+            )
+            positive = jnp.maximum(hidden_t, 0.0)
+            negative = jnp.minimum(hidden_t, 0.0)
+            relaxed_t = positive * first + negative * second
+            extra_rows.append(
+                jnp.sum(
+                    positive * first_icpt
+                    + negative * second_icpt
+                    + relaxed_t * hid_bias
+                )
+            )
+            normed_rows.append(
+                lax.dot_general(
+                    relaxed_t.astype(jnp.bfloat16),
+                    wu_full,
+                    (((0,), (0,)), ((), ())),
+                    preferred_element_type=jnp.float32,
+                )
+            )
+    normed = jnp.stack(normed_rows).reshape(2, nrows, npix, chans)
+    extra = jnp.stack(extra_rows).reshape(2, nrows)
     bias = bias + extra
-    normed = normed.reshape(2, nrows, npix, chans)
     bias = bias + jnp.sum(normed * norm_bias, axis=(2, 3))
     tilted = normed * gain
     centered = ln_scale[None, None, :, None] * (tilted - jnp.mean(tilted, axis=-1, keepdims=True))
@@ -127,10 +158,8 @@
         precision=lax.Precision.HIGHEST,
     ).reshape(2, nrows, npix, chans)
     total = coef + conv
-    box = jnp.stack([box_center, box_radius])
-    box, _ = lax.optimization_barrier((box, normed))
-    box_g = lax.all_gather(box, "spec", axis=0, tiled=False)
     box_full = box_g.transpose(1, 2, 0, 3).reshape(2, npix, nsh * cl)
+    total, box_full = lax.optimization_barrier((total, box_full))
     center, radius = box_full[0], box_full[1]
     linear = jnp.sum(total * center, axis=(2, 3))
     spread = jnp.sum(jnp.abs(total) * radius, axis=(2, 3))

time: 328 us -> 348 us (1.061); the launches traced: 328 us -> 343 us
  waiting for transfers between devices: 143 us -> 96.9 us
  matrix products: 49.5 us -> 84.8 us
  local copies, waits for them, and re-layouts: 55.5 us -> 87.8 us
  other arithmetic: 40.3 us -> 36.1 us
    all_gather x4 -> x2, waiting for transfers between devices: 141 us -> 96.8 us  [the longest x1 96.8 us: local(): gath1 = lax.all_gather(pack1, 'spec', axis=0, tiled=True)]
    dot_general x2 -> x8, matrix products: 31.7 us -> 69.9 us  [the longest x4 36.3 us: local(): lax.dot_general(wd_full, scaled16[s, r], (((1,), (1,)), ((), ())), prefer...]
    slice x2 -> x4, local copies, waits for them, and re-layouts: 2.73 us -> 31.9 us  [the longest x2 20.6 us: local(): ic = rel_g[:, 2 * npix:4 * npix].reshape(-1, 2, npix)]
    another operation x3, other arithmetic: 21.4 us -> 3.63 us  [the longest x1 2.63 us: local(): extra = jnp.stack(extra_rows).reshape(2, nrows)]
    reshape x3 -> x7, local copies, waits for them, and re-layouts: 2.09 us -> 15.5 us  [the longest x1 6.34 us: local(): ic = rel_g[:, 2 * npix:4 * npix].reshape(-1, 2, npix)]
    dot_general x1 -> x0, local copies, waits for them, and re-layouts: 7.52 us -> none  [local(): jnp.dot(relaxed16, lax.all_gather(w_up, 'spec', axis=0, tiled=True), pref...]
    add x0 -> x1, other arithmetic: none -> 4.4 us  [local(): total = coef + conv]
    transpose x0 -> x1, other arithmetic: none -> 4.4 us  [local(): box_full = box_g.transpose(1, 2, 0, 3).reshape(2, npix, nsh * cl)]
  transfers between devices with their start and end apart: 4 -> 2, of which waited for: 4 -> 1; matrix products, arithmetic and copies ran while one was open for 27% -> 35% of each run, Pallas kernels for 0% -> 0%
where the time goes in v6:
time: 348 us; the launch traced here: 343 us
  waiting for transfers between devices  96.9 us (28%)
  local copies, waits for them, and re-layouts  87.8 us (25%)
  matrix products  84.8 us (24%)
  other arithmetic  36.1 us (10%)
  blocking collectives  22.9 us (7%)
  between operations  14.8 us (4%)
    all_gather x1, waiting for transfers between devices, local(): gath1 = lax.all_gather(pack1, 'spec', axis=0, tiled=True)  96.8 us
    dot_general x4, matrix products, local(): lax.dot_general(wd_full, scaled16[s, r], (((1,), (1,)), ((), ())), prefer...  36.3 us
    dot_general x4, matrix products, local(): lax.dot_general(relaxed_t.astype(jnp.bfloat16), wu_full, (((0,), (0,)), (...  33.5 us
    all_gather x1, blocking collectives, local(): small_g = lax.all_gather(small, 'spec', axis=0, tiled=False)  22.9 us
    slice x2, local copies, waits for them, and re-layouts, local(): ic = rel_g[:, 2 * npix:4 * npix].reshape(-1, 2, npix)  20.6 us
    conv_general_dilated x1, matrix products, local(): lax.conv_general_dilated(centered.reshape(2 * nrows, MAP, MAP, chans), ta...  15 us
    convert_element_type x1, local copies, waits for them, and re-layouts, local(): box_g = gath1[:, chans + nrel:].reshape(nsh, hl * nbc)[:, :nbox].reshape(...  11.9 us
    convert_element_type x1, other arithmetic, local(): rel_g = gath1[:, chans:chans + nrel].astype(jnp.float32)  9.23 us
  transfers between devices with their start and end apart: 2, of which 1 were waited for; matrix products, arithmetic and copies ran while one was open for 35% of the time, Pallas kernels for 0%

profile of v6, /device:TPU:0, one launch (start us, length us, event | category | flops | bytes accessed | tf_op | source)
XLA Modules:
  0.0 343.4 jit_solution(17126573694595264492)
XLA Ops:
  7.2 1.0 reduce-precision_convert_fusion.1
  8.2 0.2 copy.53
  8.5 0.6 convert_element_type.41
  9.1 1.2 copy.68
  10.4 0.2 reshape.212
  10.5 1.2 copy.69
  11.8 0.2 reshape.213
  12.0 0.1 broadcast_in_dim.26
  12.1 2.1 concatenate.31
  14.2 96.8 %all-gather.5.cloned.1.call-done = bf16[4096,2103]{1,0:T(8,128)(2,1)} async-done(((bf16[256,2103]{1,0:T(8,128)(2,1)}), bf16[4096,2103]{1,0:T(8,128)(2,1)}) %all-gather.5.cloned.1.call-update) | async-done | bytes 17227792 | tf_op jit(solution)/shard_map/all_gather | solution.py:90
  111.2 22.9 %all-gather.1 = f32[16,54,64]{2,1,0:T(8,128)S(1)} all-gather(f32[1,54,64]{2,1,0:T(8,128)S(1)} %bitcast.157), channel_id=2, replica_groups=mesh['grp'=2,'spec'=16] {'spec'}, dimensions={0}, use_global_device_ids=true | all-gather | bytes 235008 | tf_op jit(solution)/shard_map/all_gather | solution.py:64
  134.1 0.1 slice_reduce_fusion.3
  134.2 0.1 mul.173
  134.3 0.1 mul.190
  134.4 0.1 mul.184
  134.6 0.1 mul.171
  134.7 0.1 copy.58
  134.8 0.2 reshape.202
  135.0 0.4 copy_bitcast_fusion
  135.5 0.9 copy-done.1
  136.4 0.3 copy-done.2
  136.7 0.7 fusion.12
  137.4 9.2 %slice_convert_fusion = f32[4096,785]{1,0:T(8,128)} fusion(bf16[4096,2103]{1,0:T(8,128)(2,1)} %all-gather.5.cloned.1.call-done), kind=kLoop, calls=%fused_computation | loop fusion | flops 3215360 | bytes 19292160 | tf_op jit(solution)/shard_map/convert_element_type | solution.py:92
  146.6 12.0 %fusion.30 = (f32[4096,392]{1,0:T(8,128)}, f32[4096,392]{1,0:T(8,128)}) fusion(f32[4096,785]{1,0:T(8,128)} %slice_convert_fusion), kind=kLoop, calls=%fused_computation.82 | loop fusion | bytes 25690112 | tf_op jit(solution)/shard_map/slice | solution.py:104
  158.6 8.6 %copy.57 = f32[4096,392]{0,1:T(8,128)} copy(f32[4096,392]{1,0:T(8,128)} %get-tuple-element.31) | data formatting | bytes 12845056 | tf_op jit(solution)/shard_map/slice | solution.py:103
  167.2 6.3 %reshape.201 = f32[4096,2,196]{0,2,1:T(8,128)} reshape(f32[4096,392]{0,1:T(8,128)} %copy.57) | data formatting | bytes 12845056 | tf_op jit(solution)/shard_map/reshape | solution.py:103
  173.5 8.6 %copy.62 = f32[4096,392]{0,1:T(8,128)} copy(f32[4096,392]{1,0:T(8,128)} %get-tuple-element.30) | data formatting | bytes 12845056 | tf_op jit(solution)/shard_map/slice | solution.py:104
  182.1 6.3 %reshape.205 = f32[4096,2,196]{0,2,1:T(8,128)} reshape(f32[4096,392]{0,1:T(8,128)} %copy.62) | data formatting | bytes 12845056 | tf_op jit(solution)/shard_map/reshape | solution.py:104
  188.4 2.8 slice_reduce_fusion
  191.2 7.9 %fusion.2 = f32[4096,196]{0,1:T(8,128)} fusion(bf16[4096,2103]{1,0:T(8,128)(2,1)} %all-gather.5.cloned.1.call-done, bf16[2,2,196,1024]{3,2,1,0:T(8,128)(2,1)S(1)} %get-tuple-element.37), kind=kOutput, calls=%fused_computation.3 | convolution fusion | flops 1644167168 | bytes 12009472 | tf_op jit(solution)/shard_map/dot_general | solution.py:118
  199.1 8.2 %fusion.4 = f32[4096,196]{0,1:T(8,128)} fusion(bf16[4096,2103]{1,0:T(8,128)(2,1)} %all-gather.5.cloned.1.call-done, bf16[2,2,196,1024]{3,2,1,0:T(8,128)(2,1)S(1)} %get-tuple-element.37), kind=kOutput, calls=%fused_computation.5 | convolution fusion | flops 1644167168 | bytes 12009472 | tf_op jit(solution)/shard_map/dot_general | solution.py:118
  207.3 8.0 %fusion = f32[4096,196]{0,1:T(8,128)} fusion(bf16[4096,2103]{1,0:T(8,128)(2,1)} %all-gather.5.cloned.1.call-done, bf16[2,2,196,1024]{3,2,1,0:T(8,128)(2,1)S(1)} %get-tuple-element.37), kind=kOutput, calls=%fused_computation.1 | convolution fusion | flops 1644167168 | bytes 12009472 | tf_op jit(solution)/shard_map/dot_general | solution.py:118
  215.3 12.2 %add_reduce_fusion.3 = (f32[]{:T(128)}, f32[]{:T(128)}, f32[]{:T(128)}, f32[]{:T(128)}, f32[4096,196]{0,1:T(8,128)}) fusion(f32[4096,2,196]{0,2,1:T(8,128)S(1)} %bitcast.154, f32[4096]{0:T(1024)S(1)} %slice_reduce_fusion, f32[4096,2,196]{0,2,1:T(8,128)S(1)} %bitcast.152, f32[4096,196]{0,1:T(8,128)} %fusion.2, f32[4096,196]{0,1:T(8,128)} %fusion, ...), kind=kOutput, calls=%fused_computation.32 | convolution fusion | flops 1679491072 | bytes 34963472 | tf_op jit(solution)/shard_map/dot_general | solution.py:118
  227.6 2.6 pad_maximum_fusion.4
  230.2 0.1 reshape.206
  230.3 5.9 %slice_convert_fusion.1 = f32[4096,294]{1,0:T(8,128)} fusion(bf16[4096,2103]{1,0:T(8,128)(2,1)} %all-gather.5.cloned.1.call-done), kind=kLoop, calls=%fused_computation.39 | loop fusion | flops 1204224 | bytes 7225344 | tf_op jit(solution)/shard_map/convert_element_type | solution.py:97
  236.2 11.9 %reshape.207 = f32[16,3,2,196,64]{4,3,2,1,0:T(8,128)} reshape(f32[4096,294]{1,0:T(8,128)} %slice_convert_fusion.1) | data formatting | bytes 9633792 | tf_op jit(solution)/shard_map/convert_element_type | solution.py:97
  248.1 4.4 %fusion.13 = f32[2,196,16,64]{3,1,0,2:T(8,128)S(1)} fusion(f32[16,3,2,196,64]{4,3,2,1,0:T(8,128)} %reshape.207), kind=kLoop, calls=%fused_computation.20 | loop fusion | flops 802816 | bytes 6422528 | tf_op jit(solution)/shard_map/transpose | solution.py:161
  252.5 2.6 copy.61
  255.1 8.3 %fusion.22 = f32[196,1024]{1,0:T(8,128)S(1)} fusion(bf16[4096,1024]{1,0:T(8,128)(2,1)} %all-gather.7.cloned.1.call-done, f32[4096,196]{0,1:T(8,128)} %get-tuple-element.45, f32[4096,2,196]{0,2,1:T(8,128)} %reshape.201), kind=kOutput, calls=%fused_computation.49 | convolution fusion | flops 1648984064 | bytes 18825216 | tf_op jit(solution)/shard_map/dot_general | solution.py:135
  263.4 1.0 stack.76
  264.4 8.5 %fusion.20 = f32[196,1024]{1,0:T(8,128)S(1)} fusion(bf16[4096,1024]{1,0:T(8,128)(2,1)} %all-gather.7.cloned.1.call-done, f32[4096,196]{0,1:T(8,128)} %fusion.4, f32[4096,2,196]{0,2,1:T(8,128)} %reshape.201), kind=kOutput, calls=%fused_computation.47 | convolution fusion | flops 1648984064 | bytes 18825216 | tf_op jit(solution)/shard_map/dot_general | solution.py:135
  272.9 1.1 stack.77
  273.9 8.4 %fusion.18 = f32[196,1024]{1,0:T(8,128)S(1)} fusion(bf16[4096,1024]{1,0:T(8,128)(2,1)} %all-gather.7.cloned.1.call-done, f32[4096,196]{0,1:T(8,128)} %fusion.2, f32[4096,2,196]{0,2,1:T(8,128)} %reshape.201), kind=kOutput, calls=%fused_computation.45 | convolution fusion | flops 1648984064 | bytes 18825216 | tf_op jit(solution)/shard_map/dot_general | solution.py:135
  282.3 1.1 stack.78
  283.5 8.4 %fusion.16 = f32[196,1024]{1,0:T(8,128)S(1)} fusion(bf16[4096,1024]{1,0:T(8,128)(2,1)} %all-gather.7.cloned.1.call-done, f32[4096,196]{0,1:T(8,128)} %fusion, f32[4096,2,196]{0,2,1:T(8,128)} %reshape.201), kind=kOutput, calls=%fused_computation.43 | convolution fusion | flops 1648984064 | bytes 18825216 | tf_op jit(solution)/shard_map/dot_general | solution.py:135
  291.9 1.0 stack.79
  292.9 0.3 multiply_reduce_fusion.4
  293.2 0.1 div.10
  293.3 1.6 multiply_reduce_fusion.3
  294.9 0.1 reduce_sum.101
  295.0 0.1 reduce_sum.103
  295.1 2.3 fusion.11
  297.4 15.0 %fusion.14 = f32[4,14,14,1024]{3,0,2,1:T(4,128)S(1)} fusion(f32[7,7,1,1024]{3,2,1,0:T(1,128)S(1)} %reshape.202, f32[4,14,14,1024]{3,2,1,0:T(8,128)S(1)} %fusion.11), kind=kOutput, calls=%fused_computation.37 | convolution fusion | flops 363528192 | bytes 6623232 | tf_op jit(solution)/shard_map/conv_general_dilated | solution.py:151
  312.4 3.9 %reshape.203 = f32[2,2,196,1024]{3,1,0,2:T(2,128)} reshape(f32[4,14,14,1024]{3,0,2,1:T(4,128)S(1)} %fusion.14) | data formatting | bytes 6422528 | tf_op jit(solution)/shard_map/reshape | solution.py:159
  316.3 4.4 %convert_add_fusion = f32[2,2,196,1024]{3,2,1,0:T(8,128)S(1)} fusion(f32[2,2,196,1024]{3,1,0,2:T(2,128)} %reshape.203, bf16[1,2,196,1024]{3,2,1,0:T(8,128)(2,1)} %copy-done.1, bf16[1,2,196,1024]{3,2,1,0:T(8,128)(2,1)} %copy-done.2), kind=kLoop, calls=%fused_computation.9 | loop fusion | flops 2408448 | bytes 8028160 | tf_op jit(solution)/shard_map/add | solution.py:160
  320.7 1.5 slice_bitcast_fusion.4
  322.2 2.5 copy.63
  324.7 2.4 copy.64
  327.1 3.6 %multiply_reduce_fusion.1 = (f32[2,2]{1,0:T(2,128)S(1)}, f32[2,2]{1,0:T(2,128)S(1)}, bf16[2,2,196,1024]{3,2,1,0:T(8,128)(2,1)}) fusion(f32[2,2,196,1024]{3,2,1,0:T(8,128)S(1)} %convert_add_fusion, f32[196,1024]{1,0:T(8,128)} %copy.63, f32[196,1024]{1,0:T(8,128)} %copy.64), kind=kLoop, calls=%fused_computation.26 | loop fusion | flops 4816888 | bytes 6422560 | tf_op jit(solution)/shard_map/reduce_sum | solution.py:164
  330.7 0.7 copy.67
  331.4 1.5 slice_bitcast_fusion.6
  332.9 1.7 copy.65
  334.6 1.7 copy.66
  (48 shorter events, 0.5 us)
Async XLA Ops:
  7.2 4.8 %copy-start.8 = (bf16[256]{0:T(256)(128)(2,1)S(1)}, bf16[256]{0:T(256)(128)(2,1)}, u32[]{:S(2)}) copy-start(bf16[256]{0:T(256)(128)(2,1)} %param.20) | copy-start | bytes 1540
  7.2 4.9 %copy-start.5 = (bf16[256,1024]{1,0:T(8,128)(2,1)S(1)}, bf16[256,1024]{1,0:T(8,128)(2,1)}, u32[]{:S(2)}) copy-start(bf16[256,1024]{1,0:T(8,128)(2,1)} %param.18) | copy-start | bytes 1572868
  7.2 103.9 %all-gather.5.cloned.1.call-start = ((), (), s32[]{:S(2)}) async-start(), calls=%async_computation | async-start | bytes 18939904 | tf_op jit(solution)/shard_map/all_gather | solution.py:90
  8.4 102.7 %copy-start.6 = (f32[49,64]{1,0:T(8,128)S(1)}, f32[49,64]{1,0:T(8,128)}, u32[]{:S(2)}) copy-start(f32[49,64]{1,0:T(8,128)} %param.26) | copy-start | bytes 37636
  8.4 102.7 %copy-start.9 = (f32[64]{0:T(128)S(1)}, f32[64]{0:T(128)}, u32[]{:S(2)}) copy-start(f32[64]{0:T(128)} %param.27) | copy-start | bytes 772
  8.5 102.7 %copy-start.10 = (f32[64]{0:T(128)S(1)}, f32[64]{0:T(128)}, u32[]{:S(2)}) copy-start(f32[64]{0:T(128)} %param.28) | copy-start | bytes 772
  8.5 102.7 %copy-start.11 = (f32[64]{0:T(128)S(1)}, f32[64]{0:T(128)}, u32[]{:S(2)}) copy-start(f32[64]{0:T(128)} %param.29) | copy-start | bytes 772
  8.5 102.7 %copy-start.12 = (f32[64]{0:T(128)S(1)}, f32[64]{0:T(128)}, u32[]{:S(2)}) copy-start(f32[64]{0:T(128)} %param.30) | copy-start | bytes 772
  8.5 102.7 %copy-start.13 = (f32[64]{0:T(128)S(1)}, f32[64]{0:T(128)}, u32[]{:S(2)}) copy-start(f32[64]{0:T(128)} %param.31) | copy-start | bytes 772
  10.4 124.2 %copy-start.7 = (f32[196]{0:T(256)S(1)}, f32[196]{0:T(256)}, u32[]{:S(2)}) copy-start(f32[196]{0:T(256)} %param.23) | copy-start | bytes 2356
  12.0 123.1 %copy-start.3 = (bf16[2,196,1024]{2,0,1:T(2,128)(2,1)S(1)}, bf16[2,196,1024]{2,0,1:T(2,128)(2,1)}, u32[]{:S(2)}) copy-start(bf16[2,196,1024]{2,0,1:T(2,128)(2,1)} %param.17) | copy-start | bytes 2408452
  12.0 123.1 %copy-start.4 = (bf16[2,196,1024]{2,0,1:T(2,128)(2,1)S(1)}, bf16[2,196,1024]{2,0,1:T(2,128)(2,1)}, u32[]{:S(2)}) copy-start(bf16[2,196,1024]{2,0,1:T(2,128)(2,1)} %param.16) | copy-start | bytes 2408452
  14.2 240.9 %all-gather.7.cloned.1.call-start = ((), (), s32[]{:S(2)}) async-start(), calls=%async_computation.1 | async-start | bytes 8912896 | tf_op jit(solution)/shard_map/all_gather | solution.py:101
  135.5 0.9 copy-start.1
  135.5 1.2 copy-start.2
  199.1 16.2 %slice-start = ((s8[6553600]{0:T(1024)(128)(4,1)}), s8[4194304]{0:T(1024)(128)(4,1)S(1)}, s32[]{:S(2)}) async-start(s8[6553600]{0:T(1024)(128)(4,1)} %bitcast.151), calls=%async_computation.2 | async-start | bytes 8388608
  199.1 16.2 %slice-start.2 = ((s8[6553600]{0:T(1024)(128)(4,1)}), s8[4194304]{0:T(1024)(128)(4,1)S(1)}, s32[]{:S(2)}) async-start(s8[6553600]{0:T(1024)(128)(4,1)} %bitcast.153), calls=%async_computation.4 | async-start | bytes 8388608
  207.3 8.0 %slice-start.1 = ((s8[6553600]{0:T(1024)(128)(4,1)}), s8[2359296]{0:T(1024)(128)(4,1)S(1)}, s32[]{:S(2)}) async-start(s8[6553600]{0:T(1024)(128)(4,1)} %bitcast.151), calls=%async_computation.3 | async-start | bytes 4718592
  207.3 8.0 %slice-start.3 = ((s8[6553600]{0:T(1024)(128)(4,1)}), s8[2359296]{0:T(1024)(128)(4,1)S(1)}, s32[]{:S(2)}) async-start(s8[6553600]{0:T(1024)(128)(4,1)} %bitcast.153), calls=%async_computation.5 | async-start | bytes 4718592
  316.3 4.4 %copy-start = (f32[2,196,16,64]{1,3,2,0:T(8,128)S(1)}, f32[2,196,16,64]{1,3,2,0:T(8,128)}, u32[]{:S(2)}) copy-start(f32[2,196,16,64]{1,3,2,0:T(8,128)} %copy.61) | copy-start | bytes 4816900
Sparse Core Ops, SparseCore 0:
  14.3 96.7 all-gather.4
  113.2 75.4 all-gather.6
